TPU v7x, 256 devices: a whole 4x4x8 slice. The times are simulated.
256 devices in a mesh: band: 16 (over z, x_hi), domain: 16 (over y, x_lo, core).
Axes of the slice: x: 4 (x_hi: 2, x_lo: 2; x = x_hi * 2 + x_lo), y: 4, z: 8, core: 2. Of those that a mesh axis runs over, the one named last changes fastest.
Arguments:
- orbitals: float32 [256, 16384], P('band', 'domain'), may hold values from -12 to 12
- potential: float32 [16384], P('domain'), may hold values from -9 to 4.5
- stencil: int32 [36, 16384], P(None, 'domain'), may hold values from 0 to 1536, as said below
- send_list: int32 [2, 4096], P(None, 'domain'), may hold values from 0 to 1023, as said below
- send_count: int32 [2, 16], P(None, 'domain'), may hold values from 0 to 256, as said below
Outputs:
- filtered: float32 [256, 16384], P('band', 'domain')
- correlation: float32 [256, 256], P('band', 'domain')
- subspace: float32 [256, 256], P('band', 'domain')
Inputs may be any that keep to these rules, and one draw needn't show every extreme that they name: `stencil`: entries below 1024 name a slot of the point's own subdomain; entries from 1024 on name only live boundary rows of an existing neighbouring subdomain; 1536 marks a neighbour outside the cluster. `send_list`: each list of 256 entries holds distinct slots of the sending subdomain. `send_count`: row 0 counts the rows subdomain d sends to d + 1, row 1 those it sends to d - 1; zero toward a missing neighbour; 256 is reached in every draw.
All inputs are finite; a program needn't handle non-finite values.
Results may differ from a plain program's by a relative error of at most 0.00015.
Values sent between devices are 32-bit elements; how exact they have to be, the bound alone decides.
No kernel may reach another device: no remote copies, remote signals or barrier semaphores. Data moves between devices by JAX's collectives and lax.ppermute only.
A program may use at most 128 MiB of HBM per device.

v0:
```python
import jax
import jax.numpy as jnp
from jax import lax
from jax.sharding import PartitionSpec as P

DEGREE = 4


WEIGHTS = (
    -5369.0 / 1800.0,
    12.0 / 7.0,
    -15.0 / 56.0,
    10.0 / 189.0,
    -1.0 / 112.0,
    2.0 / 1925.0,
    -1.0 / 16632.0,
)
KINETIC = 50.0 / 9.0
CUT_SHARE = 0.1
SPECTRAL_REACH = (
    KINETIC
    * 3.0
    * (
        abs(WEIGHTS[0])
        + 2.0
        * (
            abs(WEIGHTS[1])
            + abs(WEIGHTS[2])
            + abs(WEIGHTS[3])
            + abs(WEIGHTS[4])
            + abs(WEIGHTS[5])
            + abs(WEIGHTS[6])
        )
    )
)


def with_halo(block, sides, width):
    for axis, dim in sides:
        count = lax.axis_size(axis)
        forward = [(i, i + 1) for i in range(count - 1)]
        backward = [(target, source) for source, target in forward]
        low = lax.ppermute(
            lax.slice_in_dim(block, block.shape[dim] - width, None, axis=dim), axis, forward
        )
        high = lax.ppermute(lax.slice_in_dim(block, 0, width, axis=dim), axis, backward)
        block = jnp.concatenate([low, block, high], axis=dim)
    return block


def apply_operator(values, potential, stencil, send_list, live_slots):
    capacity = send_list.shape[1]
    sent_rows = values[:, send_list]
    sent_rows = jnp.where(live_slots[None], sent_rows, jnp.zeros_like(sent_rows))
    outgoing = jnp.concatenate([sent_rows[:, 1], sent_rows[:, 0]], axis=1)
    padded = with_halo(outgoing, (("domain", 1),), capacity)
    from_below = padded[:, :capacity]
    from_above = padded[:, 3 * capacity :]
    zero_column = jnp.zeros((values.shape[0], 1), values.dtype)
    buffer = jnp.concatenate([values, from_below, from_above, zero_column], axis=1)
    near_sum = jnp.zeros_like(values)
    for distance in range(6):
        cycle_sum = jnp.zeros_like(values)
        for member in range(6):
            cycle_sum = cycle_sum + buffer[:, stencil[6 * distance + member]]
        near_sum = near_sum + WEIGHTS[distance + 1] * cycle_sum
    return potential * values - KINETIC * (3.0 * WEIGHTS[0] * values + near_sum)


def filter_block(orbitals, operator_fn, lowest, highest):
    top_bound = highest + SPECTRAL_REACH
    cut_point = lowest + CUT_SHARE * (top_bound - lowest)
    half_width = (top_bound - cut_point) / 2.0
    centre = (top_bound + cut_point) / 2.0
    sigma_now = half_width / (lowest - centre)
    sigma_scale = 2.0 / sigma_now
    previous = orbitals
    current = sigma_now / half_width * (operator_fn(orbitals) - centre * orbitals)
    for order_index in range(2, DEGREE + 1):
        sigma_next = 1.0 / (sigma_scale - sigma_now)
        following = (
            2.0 * sigma_next / half_width * (operator_fn(current) - centre * current)
            - sigma_now * sigma_next * previous
        )
        previous = current
        current = following
        sigma_now = sigma_next
    return current


def inner_products(left_block, right_block):
    return lax.dot_general(
        left_block,
        right_block,
        (((1,), (1,)), ((), ())),
        precision=lax.Precision.HIGHEST,
        preferred_element_type=jnp.float32,
    )


def shards(orbitals, potential, stencil, send_list, send_count):
    points = orbitals.shape[1]
    capacity = send_list.shape[1]
    domain_count = lax.axis_size("domain")
    total_points = points * domain_count
    lowest = lax.pmin(jnp.min(potential), "domain")
    highest = lax.pmax(jnp.max(potential), "domain")
    live_slots = lax.broadcasted_iota(jnp.int32, (2, capacity), 1) < send_count

    def operator_fn(values):
        return apply_operator(values, potential, stencil, send_list, live_slots)

    filtered = filter_block(orbitals, operator_fn, lowest, highest)
    applied = operator_fn(filtered)
    piece_values = lax.all_gather(filtered, "band", axis=0, tiled=True)
    piece_applied = lax.all_gather(applied, "band", axis=0, tiled=True)
    correlation_part = inner_products(filtered, piece_values)
    subspace_part = inner_products(filtered, piece_applied)
    correlation_part, subspace_part = (correlation_part, subspace_part)
    correlation_sum, subspace_sum = (
        lax.psum_scatter(correlation_part, "domain", scatter_dimension=1, tiled=True),
        lax.psum_scatter(subspace_part, "domain", scatter_dimension=1, tiled=True),
    )
    return (filtered, correlation_sum / total_points, subspace_sum / total_points)


def solution(mesh):
    placed = (
        P("band", "domain"),
        P("domain"),
        P(None, "domain"),
        P(None, "domain"),
        P(None, "domain"),
    )
    return jax.shard_map(
        shards,
        mesh=mesh,
        in_specs=placed,
        out_specs=(P("band", "domain"), P("band", "domain"), P("band", "domain")),
        check_vma=False,
    )
```

profile of v0, /device:TPU:4, one launch (start us, length us, event | category | flops | bytes accessed | tf_op | source)
XLA Modules:
  0.0 1158.1 jit_solution(5905052475874954502)
XLA Ops:
  16.9 32.3 %pmax.7 = f32[]{:T(128)} all-reduce(f32[]{:T(128)} %get-tuple-element.19), channel_id=1, replica_groups=mesh['band'=16,'domain'=16] {'domain'}, use_global_device_ids=true, to_apply=%region_3.0 | all-reduce | flops 1 | bytes 8 | tf_op jit(solution)/shard_map/pmax | solution.py:107
  49.2 27.8 %pmin.7 = f32[]{:T(128)} all-reduce(f32[]{:T(128)} %get-tuple-element.18), channel_id=1, replica_groups=mesh['band'=16,'domain'=16] {'domain'}, use_global_device_ids=true, to_apply=%region_1.0 | all-reduce | flops 1 | bytes 8 | tf_op jit(solution)/shard_map/pmin | solution.py:106
  201.8 4.0 gather_fusion.54
  209.8 4.0 gather_fusion.56
  213.8 4.0 gather_fusion.57
  229.7 4.0 gather_fusion.61
  233.7 4.0 gather_fusion.62
  237.7 4.0 gather_fusion.63
  241.7 4.0 gather_fusion.64
  257.7 4.0 gather_fusion.68
  261.7 4.0 gather_fusion.69
  265.7 4.0 gather_fusion.70
  269.7 4.0 gather_fusion.71
  293.6 4.0 gather_fusion.44
  297.6 4.0 gather_fusion.45
  301.6 4.0 gather_fusion.46
  309.6 4.0 gather_fusion.48
  397.6 4.0 gather_fusion.91
  405.6 4.0 gather_fusion.93
  409.6 4.0 gather_fusion.94
  425.6 4.0 gather_fusion.98
  429.6 4.0 gather_fusion.99
  433.6 4.0 gather_fusion.100
  437.6 4.0 gather_fusion.101
  453.5 4.0 gather_fusion.105
  457.5 4.0 gather_fusion.106
  461.5 4.0 gather_fusion.107
  465.5 4.0 gather_fusion.108
  489.5 4.0 gather_fusion.81
  493.4 4.0 gather_fusion.82
  497.4 4.0 gather_fusion.83
  589.5 4.0 gather_fusion.113
  597.5 4.0 gather_fusion.129
  601.5 4.0 gather_fusion.130
  609.4 4.0 gather_fusion.132
  617.4 4.0 gather_fusion.134
  621.4 4.0 gather_fusion.135
  629.4 4.0 gather_fusion.137
  637.4 4.0 gather_fusion.139
  645.4 4.0 gather_fusion.141
  657.4 4.0 gather_fusion.144
  661.4 4.0 gather_fusion.145
  689.3 4.0 gather_fusion.119
  693.3 4.0 gather_fusion.120
  697.3 4.0 gather_fusion.121
  705.3 4.0 gather_fusion.123
  796.9 4.0 gather_fusion.169
  804.8 4.0 gather_fusion.171
  808.9 4.0 gather_fusion.172
  816.8 4.0 gather_fusion.174
  836.8 4.0 gather_fusion.179
  844.8 4.0 gather_fusion.181
  856.8 4.0 gather_fusion.151
  864.7 4.0 gather_fusion.153
  868.7 4.0 gather_fusion.154
  872.7 4.0 gather_fusion.155
  876.7 4.0 gather_fusion.156
  892.7 4.0 gather_fusion.160
  896.7 4.0 gather_fusion.161
  908.7 4.0 gather_fusion.164
  912.7 4.0 gather_fusion.183
  944.3 76.7 %all-gather.5.cloned.1.call-done = f32[256,1024]{1,0:T(8,128)} async-done(((f32[16,1024]{1,0:T(8,128)}), f32[256,1024]{1,0:T(8,128)}) %all-gather.5.cloned.1.call-update) | async-done | bytes 1048592 | tf_op jit(solution)/shard_map/all_gather | solution.py:116
  1023.9 61.8 %reduce-scatter.7.cloned.1.call-done = f32[16,16]{1,0:T(8,128)} async-done(((f32[256,16]{1,0:T(8,128)}), f32[16,16]{1,0:T(8,128)}) %reduce-scatter.7.cloned.1.call-update) | async-done | bytes 1040
  1087.1 62.9 %reduce-scatter.9.cloned.1.call-done = f32[16,16]{1,0:T(8,128)} async-done(((f32[256,16]{1,0:T(8,128)}), f32[16,16]{1,0:T(8,128)}) %reduce-scatter.9.cloned.1.call-update) | async-done | bytes 1040
  (1099 shorter events, 641.5 us)
Async XLA Ops:
  7.2 934.3 %all-gather.3.cloned.1.call-start = ((), (), s32[]{:S(2)}) async-start(), calls=%async_computation.2 | async-start | bytes 1114112 | tf_op jit(solution)/shard_map/all_gather | solution.py:115
  10.0 4.5 copy-start.327
  11.4 68.0 %collective-permute-start = (f32[16,256]{1,0:T(8,128)S(1)}, f32[16,256]{1,0:T(8,128)S(1)}, u32[]{:S(2)}, u32[]{:S(2)}) collective-permute-start(f32[16,256]{1,0:T(8,128)S(1)} %get-tuple-element.64), channel_id=1, source_target_pairs={{0,1},{1,2},{2,3},{3,4},{4,5},{5,6},{6,7},{7,8},{8,9},{9,10},{10,1... | collective-permute-start | bytes 49160 | tf_op jit(solution)/shard_map/ppermute | solution.py:43
  13.2 66.4 %collective-permute-start.1 = (f32[16,256]{1,0:T(8,128)S(1)}, f32[16,256]{1,0:T(8,128)S(1)}, u32[]{:S(2)}, u32[]{:S(2)}) collective-permute-start(f32[16,256]{1,0:T(8,128)S(1)} %get-tuple-element.65), channel_id=1, source_target_pairs={{1,0},{2,1},{3,2},{4,3},{5,4},{6,5},{7,6},{8,7},{9,8},{10,9},{11,1... | collective-permute-start | bytes 49160 | tf_op jit(solution)/shard_map/ppermute | solution.py:46
  14.7 65.3 %copy-start.149 = (s32[1024]{0:T(1024)}, s32[1024]{0:T(1024)S(1)}, u32[]{:S(2)}) copy-start(s32[1024]{0:T(1024)S(1)} %broadcast_clamp_fusion.34) | copy-start | bytes 12292
  14.7 68.2 %copy-start.154 = (s32[1024]{0:T(1024)}, s32[1024]{0:T(1024)S(1)}, u32[]{:S(2)}) copy-start(s32[1024]{0:T(1024)S(1)} %broadcast_clamp_fusion.19) | copy-start | bytes 12292
  14.8 71.2 %copy-start.159 = (s32[1024]{0:T(1024)}, s32[1024]{0:T(1024)S(1)}, u32[]{:S(2)}) copy-start(s32[1024]{0:T(1024)S(1)} %broadcast_clamp_fusion.18) | copy-start | bytes 12292
  14.8 74.2 %copy-start.164 = (s32[1024]{0:T(1024)}, s32[1024]{0:T(1024)S(1)}, u32[]{:S(2)}) copy-start(s32[1024]{0:T(1024)S(1)} %broadcast_clamp_fusion.17) | copy-start | bytes 12292
  14.8 77.1 %copy-start.169 = (s32[1024]{0:T(1024)}, s32[1024]{0:T(1024)S(1)}, u32[]{:S(2)}) copy-start(s32[1024]{0:T(1024)S(1)} %broadcast_clamp_fusion.16) | copy-start | bytes 12292
  14.8 80.1 %copy-start.174 = (s32[1024]{0:T(1024)}, s32[1024]{0:T(1024)S(1)}, u32[]{:S(2)}) copy-start(s32[1024]{0:T(1024)S(1)} %broadcast_clamp_fusion.15) | copy-start | bytes 12292
  14.9 83.1 %copy-start.179 = (s32[1024]{0:T(1024)}, s32[1024]{0:T(1024)S(1)}, u32[]{:S(2)}) copy-start(s32[1024]{0:T(1024)S(1)} %broadcast_clamp_fusion.14) | copy-start | bytes 12292
  14.9 86.0 %copy-start.184 = (s32[1024]{0:T(1024)}, s32[1024]{0:T(1024)S(1)}, u32[]{:S(2)}) copy-start(s32[1024]{0:T(1024)S(1)} %broadcast_clamp_fusion.13) | copy-start | bytes 12292
  14.9 89.0 %copy-start.189 = (s32[1024]{0:T(1024)}, s32[1024]{0:T(1024)S(1)}, u32[]{:S(2)}) copy-start(s32[1024]{0:T(1024)S(1)} %broadcast_clamp_fusion.12) | copy-start | bytes 12292
  14.9 92.0 %copy-start.194 = (s32[1024]{0:T(1024)}, s32[1024]{0:T(1024)S(1)}, u32[]{:S(2)}) copy-start(s32[1024]{0:T(1024)S(1)} %broadcast_clamp_fusion.11) | copy-start | bytes 12292
  14.9 94.9 %copy-start.199 = (s32[1024]{0:T(1024)}, s32[1024]{0:T(1024)S(1)}, u32[]{:S(2)}) copy-start(s32[1024]{0:T(1024)S(1)} %broadcast_clamp_fusion.10) | copy-start | bytes 12292
  15.0 97.9 %copy-start.204 = (s32[1024]{0:T(1024)}, s32[1024]{0:T(1024)S(1)}, u32[]{:S(2)}) copy-start(s32[1024]{0:T(1024)S(1)} %broadcast_clamp_fusion.9) | copy-start | bytes 12292
  15.0 100.9 %copy-start.209 = (s32[1024]{0:T(1024)}, s32[1024]{0:T(1024)S(1)}, u32[]{:S(2)}) copy-start(s32[1024]{0:T(1024)S(1)} %broadcast_clamp_fusion.8) | copy-start | bytes 12292
  15.0 103.8 %copy-start.214 = (s32[1024]{0:T(1024)}, s32[1024]{0:T(1024)S(1)}, u32[]{:S(2)}) copy-start(s32[1024]{0:T(1024)S(1)} %broadcast_clamp_fusion.7) | copy-start | bytes 12292
  15.0 106.8 %copy-start.219 = (s32[1024]{0:T(1024)}, s32[1024]{0:T(1024)S(1)}, u32[]{:S(2)}) copy-start(s32[1024]{0:T(1024)S(1)} %broadcast_clamp_fusion.6) | copy-start | bytes 12292
  15.1 109.8 %copy-start.224 = (s32[1024]{0:T(1024)}, s32[1024]{0:T(1024)S(1)}, u32[]{:S(2)}) copy-start(s32[1024]{0:T(1024)S(1)} %broadcast_clamp_fusion.5) | copy-start | bytes 12292
  15.1 112.7 %copy-start.229 = (s32[1024]{0:T(1024)}, s32[1024]{0:T(1024)S(1)}, u32[]{:S(2)}) copy-start(s32[1024]{0:T(1024)S(1)} %broadcast_clamp_fusion.4) | copy-start | bytes 12292
  15.1 115.7 %copy-start.234 = (s32[1024]{0:T(1024)}, s32[1024]{0:T(1024)S(1)}, u32[]{:S(2)}) copy-start(s32[1024]{0:T(1024)S(1)} %broadcast_clamp_fusion.3) | copy-start | bytes 12292
  15.1 118.7 %copy-start.239 = (s32[1024]{0:T(1024)}, s32[1024]{0:T(1024)S(1)}, u32[]{:S(2)}) copy-start(s32[1024]{0:T(1024)S(1)} %broadcast_clamp_fusion.2) | copy-start | bytes 12292
  15.1 121.6 %copy-start.244 = (s32[1024]{0:T(1024)}, s32[1024]{0:T(1024)S(1)}, u32[]{:S(2)}) copy-start(s32[1024]{0:T(1024)S(1)} %broadcast_clamp_fusion.35) | copy-start | bytes 12292
  15.2 124.6 %copy-start.249 = (s32[1024]{0:T(1024)}, s32[1024]{0:T(1024)S(1)}, u32[]{:S(2)}) copy-start(s32[1024]{0:T(1024)S(1)} %broadcast_clamp_fusion.33) | copy-start | bytes 12292
  15.2 127.6 %copy-start.254 = (s32[1024]{0:T(1024)}, s32[1024]{0:T(1024)S(1)}, u32[]{:S(2)}) copy-start(s32[1024]{0:T(1024)S(1)} %broadcast_clamp_fusion.32) | copy-start | bytes 12292
  15.2 130.5 %copy-start.259 = (s32[1024]{0:T(1024)}, s32[1024]{0:T(1024)S(1)}, u32[]{:S(2)}) copy-start(s32[1024]{0:T(1024)S(1)} %broadcast_clamp_fusion.31) | copy-start | bytes 12292
  15.2 133.5 %copy-start.264 = (s32[1024]{0:T(1024)}, s32[1024]{0:T(1024)S(1)}, u32[]{:S(2)}) copy-start(s32[1024]{0:T(1024)S(1)} %broadcast_clamp_fusion.30) | copy-start | bytes 12292
  15.3 136.5 %copy-start.269 = (s32[1024]{0:T(1024)}, s32[1024]{0:T(1024)S(1)}, u32[]{:S(2)}) copy-start(s32[1024]{0:T(1024)S(1)} %broadcast_clamp_fusion.29) | copy-start | bytes 12292
  15.3 139.4 %copy-start.274 = (s32[1024]{0:T(1024)}, s32[1024]{0:T(1024)S(1)}, u32[]{:S(2)}) copy-start(s32[1024]{0:T(1024)S(1)} %broadcast_clamp_fusion.28) | copy-start | bytes 12292
  15.3 142.4 %copy-start.279 = (s32[1024]{0:T(1024)}, s32[1024]{0:T(1024)S(1)}, u32[]{:S(2)}) copy-start(s32[1024]{0:T(1024)S(1)} %broadcast_clamp_fusion.27) | copy-start | bytes 12292
  15.3 145.4 %copy-start.284 = (s32[1024]{0:T(1024)}, s32[1024]{0:T(1024)S(1)}, u32[]{:S(2)}) copy-start(s32[1024]{0:T(1024)S(1)} %broadcast_clamp_fusion.26) | copy-start | bytes 12292
  15.4 148.3 %copy-start.289 = (s32[1024]{0:T(1024)}, s32[1024]{0:T(1024)S(1)}, u32[]{:S(2)}) copy-start(s32[1024]{0:T(1024)S(1)} %broadcast_clamp_fusion.25) | copy-start | bytes 12292
  15.4 151.3 %copy-start.294 = (s32[1024]{0:T(1024)}, s32[1024]{0:T(1024)S(1)}, u32[]{:S(2)}) copy-start(s32[1024]{0:T(1024)S(1)} %broadcast_clamp_fusion.24) | copy-start | bytes 12292
  15.4 154.3 %copy-start.299 = (s32[1024]{0:T(1024)}, s32[1024]{0:T(1024)S(1)}, u32[]{:S(2)}) copy-start(s32[1024]{0:T(1024)S(1)} %broadcast_clamp_fusion.23) | copy-start | bytes 12292
  15.4 157.2 %copy-start.304 = (s32[1024]{0:T(1024)}, s32[1024]{0:T(1024)S(1)}, u32[]{:S(2)}) copy-start(s32[1024]{0:T(1024)S(1)} %broadcast_clamp_fusion.22) | copy-start | bytes 12292
  15.4 160.2 %copy-start.309 = (s32[1024]{0:T(1024)}, s32[1024]{0:T(1024)S(1)}, u32[]{:S(2)}) copy-start(s32[1024]{0:T(1024)S(1)} %broadcast_clamp_fusion.21) | copy-start | bytes 12292
  15.5 163.2 %copy-start.314 = (s32[1024]{0:T(1024)}, s32[1024]{0:T(1024)S(1)}, u32[]{:S(2)}) copy-start(s32[1024]{0:T(1024)S(1)} %broadcast_clamp_fusion.20) | copy-start | bytes 12292
  15.5 166.8 %copy-start.319 = (s32[1024]{0:T(1024)}, s32[1024]{0:T(1024)S(1)}, u32[]{:S(2)}) copy-start(s32[1024]{0:T(1024)S(1)} %broadcast_clamp_fusion.1) | copy-start | bytes 12292
  16.2 169.7 %copy-start.324 = (s32[1024]{0:T(1024)}, s32[1024]{0:T(1024)S(1)}, u32[]{:S(2)}) copy-start(s32[1024]{0:T(1024)S(1)} %broadcast_clamp_fusion) | copy-start | bytes 12292
  192.2 3.4 collective-permute-start.2
  194.0 3.1 collective-permute-start.3
  257.7 4.0 copy-start.230
  261.7 4.0 copy-start.235
  269.7 4.0 copy-start.245
  301.6 4.0 copy-start.285
  385.9 5.5 collective-permute-start.4
  389.8 3.1 collective-permute-start.5
  457.5 4.0 copy-start.236
  465.5 4.0 copy-start.246
  497.4 4.0 copy-start.286
  581.8 5.7 collective-permute-start.6
  585.7 3.1 collective-permute-start.7
  657.4 4.0 copy-start.242
  661.4 4.0 copy-start.247
  697.3 4.0 copy-start.292
  772.2 248.8 %all-gather.5.cloned.1.call-start = ((), (), s32[]{:S(2)}) async-start(), calls=%async_computation.3 | async-start | bytes 1114112 | tf_op jit(solution)/shard_map/all_gather | solution.py:116
  775.0 5.4 collective-permute-start.8
  778.9 3.1 collective-permute-start.9
  804.8 4.0 copy-start.193
  836.8 4.0 copy-start.233
  844.8 4.0 copy-start.243
  941.4 144.4 %reduce-scatter.7.cloned.1.call-start = ((), (), s32[]{:S(2)}) async-start(), calls=%async_computation.4 | async-start | bytes 139264
  944.3 205.7 %reduce-scatter.9.cloned.1.call-start = ((), (), s32[]{:S(2)}) async-start(), calls=%async_computation.5 | async-start | bytes 139264
  (289 other events, 718.5 us)
Sparse Core Ops, SparseCore 0:
  772.3 78.6 all-gather.2
  941.5 79.5 all-gather.4
  1023.6 62.1 reduce-scatter.6
  1088.1 61.9 reduce-scatter.8
where the time goes:
time: 1170 us; the launch traced here: 1160 us
  local copies, waits for them, and re-layouts  837 us (72%)
  waiting for transfers between devices  207 us (18%)
  blocking collectives  60.1 us (5%)
  starting transfers between devices  22.8 us (2%)
  between operations  19.4 us (2%)
    gather x360, local copies, waits for them, and re-layouts, apply_operator(): cycle_sum = cycle_sum + buffer[:, stencil[6 * distance + member]]  804 us
    unnamed x6, waiting for transfers between devices  125 us
    all_gather x1, waiting for transfers between devices, shards(): piece_applied = lax.all_gather(applied, 'band', axis=0, tiled=True)  76.7 us
    pmax x1, blocking collectives, shards(): highest = lax.pmax(jnp.max(potential), 'domain')  32.3 us
    pmin x1, blocking collectives, shards(): lowest = lax.pmin(jnp.min(potential), 'domain')  27.8 us
    unnamed x682, local copies, waits for them, and re-layouts  25.6 us
  transfers between devices with their start and end apart: 14, of which 7 were waited for; matrix products, arithmetic and copies ran while one was open for 14% of the time, Pallas kernels for 0%

commit v1 on v0

v1 whole, which is shorter than its diff:
```python
import jax
import jax.numpy as jnp
from jax import lax
from jax.sharding import PartitionSpec as P

DEGREE = 4


WEIGHTS = (
    -5369.0 / 1800.0,
    12.0 / 7.0,
    -15.0 / 56.0,
    10.0 / 189.0,
    -1.0 / 112.0,
    2.0 / 1925.0,
    -1.0 / 16632.0,
)
KINETIC = 50.0 / 9.0
CUT_SHARE = 0.1
SPECTRAL_REACH = (
    KINETIC
    * 3.0
    * (
        abs(WEIGHTS[0])
        + 2.0
        * (
            abs(WEIGHTS[1])
            + abs(WEIGHTS[2])
            + abs(WEIGHTS[3])
            + abs(WEIGHTS[4])
            + abs(WEIGHTS[5])
            + abs(WEIGHTS[6])
        )
    )
)


def dense(left, right):
    return lax.dot_general(
        left,
        right,
        (((1,), (0,)), ((), ())),
        precision=lax.Precision.HIGHEST,
        preferred_element_type=jnp.float32,
    )


def stencil_matrix(stencil, rows):
    slots = lax.broadcasted_iota(jnp.int32, (rows, stencil.shape[1]), 0)
    total = jnp.zeros((rows, stencil.shape[1]), jnp.float32)
    for distance in range(6):
        count = jnp.zeros((rows, stencil.shape[1]), jnp.float32)
        for member in range(6):
            count = count + (slots == stencil[6 * distance + member][None, :]).astype(jnp.float32)
        total = total + WEIGHTS[distance + 1] * count
    return total


def selection_matrix(send_list, live_slots, points):
    slots = lax.broadcasted_iota(jnp.int32, (points, send_list.shape[1]), 0)
    down = (slots == send_list[1][None, :]) & live_slots[1][None, :]
    up = (slots == send_list[0][None, :]) & live_slots[0][None, :]
    return jnp.concatenate([down, up], axis=1).astype(jnp.float32)


def apply_operator(values, potential, pick, near_local, near_below, near_above):
    capacity = pick.shape[1] // 2
    count = lax.axis_size("domain")
    outgoing = dense(values, pick)
    forward = [(i, i + 1) for i in range(count - 1)]
    backward = [(i + 1, i) for i in range(count - 1)]
    from_below = lax.ppermute(outgoing[:, capacity:], "domain", forward)
    from_above = lax.ppermute(outgoing[:, :capacity], "domain", backward)
    near_sum = dense(values, near_local) + dense(from_below, near_below) + dense(from_above, near_above)
    return potential * values - KINETIC * (3.0 * WEIGHTS[0] * values + near_sum)


def filter_block(orbitals, operator_fn, lowest, highest):
    top_bound = highest + SPECTRAL_REACH
    cut_point = lowest + CUT_SHARE * (top_bound - lowest)
    half_width = (top_bound - cut_point) / 2.0
    centre = (top_bound + cut_point) / 2.0
    sigma_now = half_width / (lowest - centre)
    sigma_scale = 2.0 / sigma_now
    previous = orbitals
    current = sigma_now / half_width * (operator_fn(orbitals) - centre * orbitals)
    for order_index in range(2, DEGREE + 1):
        sigma_next = 1.0 / (sigma_scale - sigma_now)
        following = (
            2.0 * sigma_next / half_width * (operator_fn(current) - centre * current)
            - sigma_now * sigma_next * previous
        )
        previous = current
        current = following
        sigma_now = sigma_next
    return current


def inner_products(left_block, right_block):
    return lax.dot_general(
        left_block,
        right_block,
        (((1,), (1,)), ((), ())),
        precision=lax.Precision.HIGHEST,
        preferred_element_type=jnp.float32,
    )


def shards(orbitals, potential, stencil, send_list, send_count):
    rows, points = orbitals.shape
    capacity = send_list.shape[1]
    domain_count = lax.axis_size("domain")
    band_count = lax.axis_size("band")
    total_points = points * domain_count
    extremes = lax.pmax(jnp.stack([-jnp.min(potential), jnp.max(potential)]), "domain")
    lowest = -extremes[0]
    highest = extremes[1]
    live_slots = lax.broadcasted_iota(jnp.int32, (2, capacity), 1) < send_count

    pick = selection_matrix(send_list, live_slots, points)
    weight = stencil_matrix(stencil, points + 2 * capacity)
    near_local = weight[:points]
    near_below = weight[points : points + capacity]
    near_above = weight[points + capacity :]

    def operator_fn(values):
        return apply_operator(values, potential, pick, near_local, near_below, near_above)

    filtered = filter_block(orbitals, operator_fn, lowest, highest)
    applied = operator_fn(filtered)
    both = jnp.stack([filtered, applied])
    gathered = lax.all_gather(both, "band", axis=1, tiled=False)
    gathered = gathered.reshape(2, band_count * rows, points)
    parts = jnp.stack(
        [inner_products(filtered, gathered[0]), inner_products(filtered, gathered[1])]
    )
    sums = lax.psum_scatter(parts, "domain", scatter_dimension=2, tiled=True)
    return (filtered, sums[0] / total_points, sums[1] / total_points)


def solution(mesh):
    placed = (
        P("band", "domain"),
        P("domain"),
        P(None, "domain"),
        P(None, "domain"),
        P(None, "domain"),
    )
    return jax.shard_map(
        shards,
        mesh=mesh,
        in_specs=placed,
        out_specs=(P("band", "domain"), P("band", "domain"), P("band", "domain")),
        check_vma=False,
    )
```

time: 1170 us -> 293 us (0.25)
  local copies, waits for them, and re-layouts: 837 us -> 8.71 us
  waiting for transfers between devices: 207 us -> 156 us
  blocking collectives: 60.1 us -> 31.7 us
  matrix products: 5.66 us -> 29.9 us
  other arithmetic: 5.84 us -> 29.3 us
    gather x370 -> x0, local copies, waits for them, and re-layouts: 809 us -> none  [the longest x360 804 us: apply_operator(): cycle_sum = cycle_sum + buffer[:, stencil[6 * distance + member]]]
    unnamed x6 -> x3, waiting for transfers between devices: 125 us -> 62.6 us
    dot_general x0 -> x22, matrix products: none -> 29.9 us  [the longest x20 25.6 us: dense(): lax.dot_general(left, right, (((1,), (0,)), ((), ())), precision=lax.Prec...]
    pmin x1 -> x0, blocking collectives: 27.8 us -> none  [shards(): lowest = lax.pmin(jnp.min(potential), 'domain')]
    add x0 -> x1, other arithmetic: none -> 24.2 us  [stencil_matrix(): total = total + WEIGHTS[distance + 1] * count]
    unnamed x682 -> x15, local copies, waits for them, and re-layouts: 25.6 us -> 4.59 us
    all_gather x2 -> x1, waiting for transfers between devices: 76.7 us -> 89 us  [shards(): gathered = lax.all_gather(both, 'band', axis=1, tiled=False)]
  transfers between devices with their start and end apart: 14 -> 12, of which waited for: 7 -> 6; matrix products, arithmetic and copies ran while one was open for 14% -> 16% of each run, Pallas kernels for 0% -> 0%
where the time goes in v1:
time: 293 us; the launch traced here: 292 us
  waiting for transfers between devices  156 us (53%)
  blocking collectives  31.7 us (11%)
  matrix products  29.9 us (10%)
  other arithmetic  29.3 us (10%)
  starting transfers between devices  19.8 us (7%)
  between operations  16.6 us (6%)
  local copies, waits for them, and re-layouts  8.71 us (3%)
    all_gather x1, waiting for transfers between devices, shards(): gathered = lax.all_gather(both, 'band', axis=1, tiled=False)  89 us
    unnamed x3, waiting for transfers between devices  62.6 us
    pmax x1, blocking collectives, shards(): lax.pmax(jnp.stack([-jnp.min(potential), jnp.max(potential)]), 'domain')  31.7 us
    dot_general x20, matrix products, dense(): lax.dot_general(left, right, (((1,), (0,)), ((), ())), precision=lax.Prec...  25.6 us
    add x1, other arithmetic, stencil_matrix(): total = total + WEIGHTS[distance + 1] * count  24.2 us
    ppermute x5, starting transfers between devices, apply_operator(): from_below = lax.ppermute(outgoing[:, capacity:], 'domain', forward)  13.3 us
    ppermute x5, starting transfers between devices, apply_operator(): from_above = lax.ppermute(outgoing[:, :capacity], 'domain', backward)  6.42 us
  transfers between devices with their start and end apart: 12, of which 6 were waited for; matrix products, arithmetic and copies ran while one was open for 16% of the time, Pallas kernels for 0%

profile of v1, /device:TPU:4, one launch (start us, length us, event | category | flops | bytes accessed | tf_op | source)
XLA Modules:
  0.0 292.3 jit_solution(6034697713342527034)
XLA Ops:
  7.2 0.0 all-gather.3.cloned.1.call-start
  7.2 0.7 iota_compare_fusion.38
  8.0 0.8 fusion.63
  8.7 0.4 fusion.41
  9.1 0.1 pad_add_fusion
  9.2 1.5 convolution_bitcast_fusion
  10.7 1.7 collective-permute-start
  12.4 1.3 collective-permute-start.1
  13.7 1.3 fusion.54
  15.7 1.4 fusion.55
  17.1 0.7 pad_maximum_fusion.2
  17.8 1.3 fusion.56
  19.1 31.7 %pmax.7 = f32[2]{0:T(128)S(1)} all-reduce(f32[2]{0:T(128)S(1)} %pad_maximum_fusion.2), channel_id=1, replica_groups=mesh['band'=16,'domain'=16] {'domain'}, use_global_device_ids=true, to_apply=%region_2.0 | all-reduce | flops 2 | bytes 16 | tf_op jit(solution)/shard_map/pmax | solution.py:115
  50.8 24.2 %multiply_add_fusion = f32[1536,1024]{1,0:T(8,128)S(1)} fusion(s32[1024]{0:T(1024)S(1)} %bitcast.130, s32[1024]{0:T(1024)S(1)} %bitcast.131, s32[1024]{0:T(1024)S(1)} %bitcast.97, s32[1024]{0:T(1024)S(1)} %bitcast.98, s32[1024]{0:T(1024)S(1)} %bitcast.99, s32[1024]{0:T(1024)S(1)} %bitcast.100, s32[1024]{0:T(1024)S(1)} %bitcast.101, s32[1024]{0:T(1024)S(1)} %bitcast.102, ...), kind=kLoop, calls=%fused_computation | loop fusion | flops 177733632 | bytes 6438912 | tf_op jit(solution)/shard_map/add | solution.py:55
  75.0 2.7 copy-done
  77.7 2.3 fusion.10
  80.0 0.6 fusion.64
  82.2 2.0 fusion.47
  84.2 0.0 copy-done.4
  84.2 2.0 fusion.31
  86.2 0.6 fusion.65
  86.8 1.3 collective-permute-start.2
  88.1 4.3 %fusion.6 = f32[16,1024]{1,0:T(8,128)S(1)} fusion(f32[16,1024]{1,0:T(8,128)S(1)} %fusion.31, f32[1536,1024]{1,0:T(8,128)} %copy-done), kind=kOutput, calls=%fused_computation.43 | convolution fusion | flops 201326592 | bytes 4325376 | tf_op jit(solution)/shard_map/dot_general | solution.py:39
  92.4 1.3 collective-permute-start.3
  93.7 0.6 convolution_add_fusion.7
  94.3 1.1 collective-permute-done.3
  95.5 0.6 fusion.34
  96.1 0.6 fusion.66
  96.7 2.5 collective-permute-start.4
  99.2 2.1 fusion.4
  101.3 1.3 collective-permute-start.5
  102.6 0.6 convolution_add_fusion.5
  103.2 1.2 collective-permute-done.5
  104.4 0.6 fusion.37
  105.0 0.6 fusion.67
  105.6 3.9 %collective-permute-start.6 = (f32[16,256]{1,0:T(8,128)S(1)}, f32[16,256]{1,0:T(8,128)S(1)}, u32[]{:S(2)}, u32[]{:S(2)}) collective-permute-start(f32[16,256]{1,0:T(8,128)S(1)} %get-tuple-element.46), channel_id=1, source_target_pairs={{0,1},{1,2},{2,3},{3,4},{4,5},{5,6},{6,7},{7,8},{8,9},{9,10},{10,1... | collective-permute-start | bytes 49160 | tf_op jit(solution)/shard_map/ppermute | solution.py:72
  109.5 2.1 fusion.2
  111.6 1.3 collective-permute-start.7
  112.9 0.6 convolution_add_fusion.3
  113.5 1.2 collective-permute-done.7
  114.7 0.6 fusion.40
  115.3 0.0 copy-start.2
  115.3 0.6 fusion.68
  116.0 3.9 %collective-permute-start.8 = (f32[16,256]{1,0:T(8,128)S(1)}, f32[16,256]{1,0:T(8,128)S(1)}, u32[]{:S(2)}, u32[]{:S(2)}) collective-permute-start(f32[16,256]{1,0:T(8,128)S(1)} %get-tuple-element.44), channel_id=1, source_target_pairs={{0,1},{1,2},{2,3},{3,4},{4,5},{5,6},{6,7},{7,8},{8,9},{9,10},{10,1... | collective-permute-start | bytes 49160 | tf_op jit(solution)/shard_map/ppermute | solution.py:72
  119.9 2.1 fusion
  122.0 1.3 collective-permute-start.9
  123.3 0.6 convolution_add_fusion.1
  123.9 1.2 collective-permute-done.9
  125.0 0.6 fusion.16
  125.7 0.7 pad_maximum_fusion
  126.3 0.0 all-gather.3.cloned.1.call-update
  126.3 0.0 reduce-scatter.4.cloned.1.call-start
  126.4 89.0 %all-gather.3.cloned.1.call-done = f32[2,256,1024]{2,1,0:T(8,128)} async-done(((f32[2,16,1024]{2,1,0:T(8,128)}), f32[2,256,1024]{2,1,0:T(8,128)}) %all-gather.3.cloned.1.call-update) | async-done | bytes 2097168 | tf_op jit(solution)/shard_map/all_gather | solution.py:132
  215.4 2.1 convolution_bitcast_fusion.2
  217.5 2.2 convolution_bitcast_fusion.1
  219.7 0.1 copy.8
  219.8 0.8 reshape.24
  220.7 0.0 reduce-scatter.4.cloned.1.call-update
  220.7 62.6 %reduce-scatter.4.cloned.1.call-done = f32[16,32]{1,0:T(8,128)} async-done(((f32[256,32]{1,0:T(8,128)}), f32[16,32]{1,0:T(8,128)}) %reduce-scatter.4.cloned.1.call-update) | async-done | bytes 2064
  283.3 0.8 reshape.25
  284.1 0.1 copy.11
  284.1 0.6 multiply_bitcast_fusion
  284.8 0.1 copy.10
  284.8 0.6 multiply_bitcast_fusion.1
  (21 shorter events, 0.1 us)
Async XLA Ops:
  7.2 70.5 %copy-start.3 = (f32[16,1024]{1,0:T(8,128)S(1)}, f32[16,1024]{1,0:T(8,128)}, u32[]{:S(2)}) copy-start(f32[16,1024]{1,0:T(8,128)} %param.5) | copy-start | bytes 196612
  7.2 208.2 %all-gather.3.cloned.1.call-start = ((), (), s32[]{:S(2)}) async-start(), calls=%async_computation.1 | async-start | bytes 2228224 | tf_op jit(solution)/shard_map/all_gather | solution.py:132
  10.7 73.6 %copy-start.4 = (f32[1024]{0:T(1024)S(1)}, f32[1024]{0:T(1024)}, u32[]{:S(2)}) copy-start(f32[1024]{0:T(1024)} %param.6) | copy-start | bytes 12292
  10.7 73.5 %collective-permute-start = (f32[16,256]{1,0:T(8,128)S(1)}, f32[16,256]{1,0:T(8,128)S(1)}, u32[]{:S(2)}, u32[]{:S(2)}) collective-permute-start(f32[16,256]{1,0:T(8,128)S(1)} %get-tuple-element.51), channel_id=1, source_target_pairs={{0,1},{1,2},{2,3},{3,4},{4,5},{5,6},{6,7},{7,8},{8,9},{9,10},{10,1... | collective-permute-start | bytes 49160 | tf_op jit(solution)/shard_map/ppermute | solution.py:72
  12.4 69.8 %collective-permute-start.1 = (f32[16,256]{1,0:T(8,128)S(1)}, f32[16,256]{1,0:T(8,128)S(1)}, u32[]{:S(2)}, u32[]{:S(2)}) collective-permute-start(f32[16,256]{1,0:T(8,128)S(1)} %get-tuple-element.52), channel_id=1, source_target_pairs={{1,0},{2,1},{3,2},{4,3},{5,4},{6,5},{7,6},{8,7},{9,8},{10,9},{11,1... | collective-permute-start | bytes 49160 | tf_op jit(solution)/shard_map/ppermute | solution.py:73
  75.0 2.7 copy-start
  82.2 11.5 %copy-start.1 = (f32[1536,1024]{1,0:T(8,128)S(1)}, f32[1536,1024]{1,0:T(8,128)}, u32[]{:S(2)}) copy-start(f32[1536,1024]{1,0:T(8,128)} %copy-done) | copy-start | bytes 18874372
  86.8 6.9 %collective-permute-start.2 = (f32[16,256]{1,0:T(8,128)S(1)}, f32[16,256]{1,0:T(8,128)S(1)}, u32[]{:S(2)}, u32[]{:S(2)}) collective-permute-start(f32[16,256]{1,0:T(8,128)S(1)} %get-tuple-element.50), channel_id=1, source_target_pairs={{0,1},{1,2},{2,3},{3,4},{4,5},{5,6},{6,7},{7,8},{8,9},{9,10},{10,1... | collective-permute-start | bytes 49160 | tf_op jit(solution)/shard_map/ppermute | solution.py:72
  92.4 3.1 %collective-permute-start.3 = (f32[16,256]{1,0:T(8,128)S(1)}, f32[16,256]{1,0:T(8,128)S(1)}, u32[]{:S(2)}, u32[]{:S(2)}) collective-permute-start(f32[16,256]{1,0:T(8,128)S(1)} %get-tuple-element.49), channel_id=1, source_target_pairs={{1,0},{2,1},{3,2},{4,3},{5,4},{6,5},{7,6},{8,7},{9,8},{10,9},{11,1... | collective-permute-start | bytes 49160 | tf_op jit(solution)/shard_map/ppermute | solution.py:73
  96.7 5.9 %collective-permute-start.4 = (f32[16,256]{1,0:T(8,128)S(1)}, f32[16,256]{1,0:T(8,128)S(1)}, u32[]{:S(2)}, u32[]{:S(2)}) collective-permute-start(f32[16,256]{1,0:T(8,128)S(1)} %get-tuple-element.48), channel_id=1, source_target_pairs={{0,1},{1,2},{2,3},{3,4},{4,5},{5,6},{6,7},{7,8},{8,9},{9,10},{10,1... | collective-permute-start | bytes 49160 | tf_op jit(solution)/shard_map/ppermute | solution.py:72
  101.3 3.1 %collective-permute-start.5 = (f32[16,256]{1,0:T(8,128)S(1)}, f32[16,256]{1,0:T(8,128)S(1)}, u32[]{:S(2)}, u32[]{:S(2)}) collective-permute-start(f32[16,256]{1,0:T(8,128)S(1)} %get-tuple-element.47), channel_id=1, source_target_pairs={{1,0},{2,1},{3,2},{4,3},{5,4},{6,5},{7,6},{8,7},{9,8},{10,9},{11,1... | collective-permute-start | bytes 49160 | tf_op jit(solution)/shard_map/ppermute | solution.py:73
  105.6 7.3 %collective-permute-start.6 = (f32[16,256]{1,0:T(8,128)S(1)}, f32[16,256]{1,0:T(8,128)S(1)}, u32[]{:S(2)}, u32[]{:S(2)}) collective-permute-start(f32[16,256]{1,0:T(8,128)S(1)} %get-tuple-element.46), channel_id=1, source_target_pairs={{0,1},{1,2},{2,3},{3,4},{4,5},{5,6},{6,7},{7,8},{8,9},{9,10},{10,1... | collective-permute-start | bytes 49160 | tf_op jit(solution)/shard_map/ppermute | solution.py:72
  111.6 3.1 %collective-permute-start.7 = (f32[16,256]{1,0:T(8,128)S(1)}, f32[16,256]{1,0:T(8,128)S(1)}, u32[]{:S(2)}, u32[]{:S(2)}) collective-permute-start(f32[16,256]{1,0:T(8,128)S(1)} %get-tuple-element.45), channel_id=1, source_target_pairs={{1,0},{2,1},{3,2},{4,3},{5,4},{6,5},{7,6},{8,7},{9,8},{10,9},{11,1... | collective-permute-start | bytes 49160 | tf_op jit(solution)/shard_map/ppermute | solution.py:73
  115.3 170.1 %copy-start.2 = (f32[16,1024]{1,0:T(8,128)}, f32[16,1024]{1,0:T(8,128)S(1)}, u32[]{:S(2)}) copy-start(f32[16,1024]{1,0:T(8,128)S(1)} %fusion.40) | copy-start | bytes 196612
  116.0 7.3 %collective-permute-start.8 = (f32[16,256]{1,0:T(8,128)S(1)}, f32[16,256]{1,0:T(8,128)S(1)}, u32[]{:S(2)}, u32[]{:S(2)}) collective-permute-start(f32[16,256]{1,0:T(8,128)S(1)} %get-tuple-element.44), channel_id=1, source_target_pairs={{0,1},{1,2},{2,3},{3,4},{4,5},{5,6},{6,7},{7,8},{8,9},{9,10},{10,1... | collective-permute-start | bytes 49160 | tf_op jit(solution)/shard_map/ppermute | solution.py:72
  122.0 3.1 %collective-permute-start.9 = (f32[16,256]{1,0:T(8,128)S(1)}, f32[16,256]{1,0:T(8,128)S(1)}, u32[]{:S(2)}, u32[]{:S(2)}) collective-permute-start(f32[16,256]{1,0:T(8,128)S(1)} %get-tuple-element.43), channel_id=1, source_target_pairs={{1,0},{2,1},{3,2},{4,3},{5,4},{6,5},{7,6},{8,7},{9,8},{10,9},{11,1... | collective-permute-start | bytes 49160 | tf_op jit(solution)/shard_map/ppermute | solution.py:73
  126.3 156.9 %reduce-scatter.4.cloned.1.call-start = ((), (), s32[]{:S(2)}) async-start(), calls=%async_computation.2 | async-start | bytes 139264
Sparse Core Ops, SparseCore 0:
  126.5 88.8 all-gather.2
  220.8 62.4 reduce-scatter.3

commit v2 on v1

--- a/solution.py
+++ b/solution.py
@@ -106,13 +106,52 @@
     )
 
 
+def exchange(value, axis, step):
+    count = lax.axis_size(axis)
+    return lax.ppermute(value, axis, [(i, i ^ step) for i in range(count)])
+
+
+def butterfly_max(value, axis):
+    step = 1
+    while step < lax.axis_size(axis):
+        value = jnp.maximum(value, exchange(value, axis, step))
+        step *= 2
+    return value
+
+
+def gather_blocks(block, axis, steps):
+    index = lax.axis_index(axis)
+    gathered = block
+    for step in steps:
+        received = exchange(gathered, axis, step)
+        high = (index & step) != 0
+        gathered = jnp.stack(
+            [jnp.where(high, received, gathered), jnp.where(high, gathered, received)]
+        )
+    return gathered
+
+
+def scatter_sum(parts, axis, steps):
+    index = lax.axis_index(axis)
+    current = parts
+    for position, step in enumerate(steps):
+        high = (index & step) != 0
+        low_half = lax.index_in_dim(current, 0, axis=position + 1, keepdims=False)
+        high_half = lax.index_in_dim(current, 1, axis=position + 1, keepdims=False)
+        keep = jnp.where(high, high_half, low_half)
+        send = jnp.where(high, low_half, high_half)
+        current = keep + exchange(send, axis, step)
+        current = jnp.expand_dims(current, position + 1)
+    return current
+
+
 def shards(orbitals, potential, stencil, send_list, send_count):
     rows, points = orbitals.shape
     capacity = send_list.shape[1]
     domain_count = lax.axis_size("domain")
     band_count = lax.axis_size("band")
     total_points = points * domain_count
-    extremes = lax.pmax(jnp.stack([-jnp.min(potential), jnp.max(potential)]), "domain")
+    extremes = butterfly_max(jnp.stack([-jnp.min(potential), jnp.max(potential)]), "domain")
     lowest = -extremes[0]
     highest = extremes[1]
     live_slots = lax.broadcasted_iota(jnp.int32, (2, capacity), 1) < send_count
@@ -129,12 +168,17 @@
     filtered = filter_block(orbitals, operator_fn, lowest, highest)
     applied = operator_fn(filtered)
     both = jnp.stack([filtered, applied])
-    gathered = lax.all_gather(both, "band", axis=1, tiled=False)
-    gathered = gathered.reshape(2, band_count * rows, points)
-    parts = jnp.stack(
-        [inner_products(filtered, gathered[0]), inner_products(filtered, gathered[1])]
+    band_steps = (8, 4, 1, 2)
+    gathered = gather_blocks(both, "band", band_steps)
+    parts = jnp.einsum(
+        "rq,abcdsjq->srdcabj",
+        filtered,
+        gathered,
+        precision=lax.Precision.HIGHEST,
+        preferred_element_type=jnp.float32,
     )
-    sums = lax.psum_scatter(parts, "domain", scatter_dimension=2, tiled=True)
+    parts = jnp.transpose(parts, (0, 1, 5, 4, 3, 2, 6)).reshape(2 * rows, 2, 2, 2, 2, rows)
+    sums = scatter_sum(parts, "domain", (1, 2, 4, 8)).reshape(2, rows, rows)
     return (filtered, sums[0] / total_points, sums[1] / total_points)
 
 

time: 293 us -> 198 us (0.68)
  waiting for transfers between devices: 156 us -> 71.1 us
  starting transfers between devices: 19.8 us -> 56.4 us
  blocking collectives: 31.7 us -> 0 us
  between operations: 16.6 us -> 3.38 us
    all_gather x1 -> x0, waiting for transfers between devices: 89 us -> none  [shards(): gathered = lax.all_gather(both, 'band', axis=1, tiled=False)]
    ppermute x0 -> x12, waiting for transfers between devices: none -> 66 us  [exchange(): return lax.ppermute(value, axis, [(i, i ^ step) for i in range(count)])]
    unnamed x3 -> x0, waiting for transfers between devices: 62.6 us -> none
    pmax x1 -> x0, blocking collectives: 31.7 us -> none  [shards(): lax.pmax(jnp.stack([-jnp.min(potential), jnp.max(potential)]), 'domain')]
    ppermute x0 -> x12, starting transfers between devices: none -> 30.7 us  [exchange(): return lax.ppermute(value, axis, [(i, i ^ step) for i in range(count)])]
    ppermute x5, starting transfers between devices: 13.3 us -> 18.8 us  [apply_operator(): from_below = lax.ppermute(outgoing[:, capacity:], 'domain', forward)]
  transfers between devices with their start and end apart: 12 -> 22, of which waited for: 6 -> 15; matrix products, arithmetic and copies ran while one was open for 16% -> 25% of each run, Pallas kernels for 0% -> 0%
where the time goes in v2:
time: 198 us; the launch traced here: 196 us
  waiting for transfers between devices  71.1 us (36%)
  starting transfers between devices  56.4 us (28%)
  other arithmetic  29.6 us (15%)
  matrix products  27.4 us (14%)
  local copies, waits for them, and re-layouts  8.42 us (4%)
  between operations  3.38 us (2%)
    ppermute x12, waiting for transfers between devices, exchange(): return lax.ppermute(value, axis, [(i, i ^ step) for i in range(count)])  66 us
    ppermute x12, starting transfers between devices, exchange(): return lax.ppermute(value, axis, [(i, i ^ step) for i in range(count)])  30.7 us
    dot_general x20, matrix products, dense(): lax.dot_general(left, right, (((1,), (0,)), ((), ())), precision=lax.Prec...  25.6 us
    add x1, other arithmetic, stencil_matrix(): total = total + WEIGHTS[distance + 1] * count  24.2 us
    ppermute x5, starting transfers between devices, apply_operator(): from_below = lax.ppermute(outgoing[:, capacity:], 'domain', forward)  18.8 us
    ppermute x5, starting transfers between devices, apply_operator(): from_above = lax.ppermute(outgoing[:, :capacity], 'domain', backward)  6.82 us
    ppermute x5, waiting for transfers between devices, apply_operator(): from_above = lax.ppermute(outgoing[:, :capacity], 'domain', backward)  5.1 us
    unnamed x12, local copies, waits for them, and re-layouts  3.98 us
  transfers between devices with their start and end apart: 22, of which 15 were waited for; matrix products, arithmetic and copies ran while one was open for 25% of the time, Pallas kernels for 0%

profile of v2, /device:TPU:4, one launch (start us, length us, event | category | flops | bytes accessed | tf_op | source)
XLA Modules:
  0.0 196.2 jit_solution(6138397580036752615)
XLA Ops:
  0.6 1.3 fusion.68
  2.6 0.7 pad_maximum_fusion.4
  3.4 0.7 iota_compare_fusion.38
  4.1 0.8 fusion.76
  5.4 1.5 convolution_bitcast_fusion
  6.8 2.4 %collective-permute-start.4 = (f32[16,256]{1,0:T(8,128)S(1)}, f32[16,256]{1,0:T(8,128)S(1)}, u32[]{:S(2)}, u32[]{:S(2)}) collective-permute-start(f32[16,256]{1,0:T(8,128)S(1)} %get-tuple-element.62), channel_id=1, source_target_pairs={{0,1},{1,2},{2,3},{3,4},{4,5},{5,6},{6,7},{7,8},{8,9},{9,10},{10,1... | collective-permute-start | bytes 49160 | tf_op jit(solution)/shard_map/ppermute | solution.py:72
  9.3 1.3 collective-permute-start.5
  10.6 1.3 fusion.70
  11.9 1.4 fusion.69
  13.3 24.2 %multiply_add_fusion = f32[1536,1024]{1,0:T(8,128)S(1)} fusion(s32[1024]{0:T(1024)S(1)} %bitcast.149, s32[1024]{0:T(1024)S(1)} %bitcast.150, s32[1024]{0:T(1024)S(1)} %bitcast.152, s32[1024]{0:T(1024)S(1)} %bitcast.153, s32[1024]{0:T(1024)S(1)} %bitcast.154, s32[1024]{0:T(1024)S(1)} %bitcast.155, s32[1024]{0:T(1024)S(1)} %bitcast.156, s32[1024]{0:T(1024)S(1)} %bitcast.157, ...), kind=kLoop, calls=%fused_computation | loop fusion | flops 177733632 | bytes 6438912 | tf_op jit(solution)/shard_map/add | solution.py:55
  37.5 2.6 %copy-done = f32[1536,1024]{1,0:T(8,128)} copy-done((f32[1536,1024]{1,0:T(8,128)}, f32[1536,1024]{1,0:T(8,128)S(1)}, u32[]{:S(2)}) %copy-start) | copy-done | bytes 6291480
  40.1 2.3 %fusion.17 = f32[16,1024]{1,0:T(8,128)S(1)} fusion(f32[16,1024]{1,0:T(8,128)S(1)} %copy-done.3, f32[1536,1024]{1,0:T(8,128)S(1)} %multiply_add_fusion), kind=kOutput, calls=%fused_computation.53 | convolution fusion | flops 201326592 | bytes 4325376 | tf_op jit(solution)/shard_map/dot_general | solution.py:39
  42.4 0.7 fusion.107
  43.1 3.1 %collective-permute-start.1 = (f32[2]{0:T(128)S(1)}, f32[2]{0:T(128)S(1)}, u32[]{:S(2)}, u32[]{:S(2)}) collective-permute-start(f32[2]{0:T(128)S(1)} %fusion.107), channel_id=1, source_target_pairs={{0,2},{1,3},{2,0},{3,1},{4,6},{5,7},{6,4},{7,5},{8,10},{9,11},{10,... | collective-permute-start | bytes 32 | tf_op jit(solution)/shard_map/ppermute | solution.py:111
  46.2 1.5 collective-permute-done.1
  47.8 0.7 fusion.108
  48.5 3.3 %collective-permute-start.2 = (f32[2]{0:T(128)S(1)}, f32[2]{0:T(128)S(1)}, u32[]{:S(2)}, u32[]{:S(2)}) collective-permute-start(f32[2]{0:T(128)S(1)} %fusion.108), channel_id=1, source_target_pairs={{0,4},{1,5},{2,6},{3,7},{4,0},{5,1},{6,2},{7,3},{8,12},{9,13},{10,... | collective-permute-start | bytes 32 | tf_op jit(solution)/shard_map/ppermute | solution.py:111
  51.8 1.5 collective-permute-done.2
  53.4 3.6 %collective-permute-start.3 = (f32[2]{0:T(128)S(1)}, f32[2]{0:T(128)S(1)}, u32[]{:S(2)}, u32[]{:S(2)}) collective-permute-start(f32[2]{0:T(128)S(1)} %max.14), channel_id=1, source_target_pairs={{0,8},{1,9},{2,10},{3,11},{4,12},{5,13},{6,14},{7,15},{8,0},{9,1},... | collective-permute-start | bytes 32 | tf_op jit(solution)/shard_map/ppermute | solution.py:111
  57.0 1.5 collective-permute-done.3
  60.9 2.0 %fusion.54 = f32[16,1024]{1,0:T(8,128)S(1)} fusion(f32[16,256]{1,0:T(8,128)S(1)} %collective-permute-done.5, f32[1536,1024]{1,0:T(8,128)} %copy-done), kind=kOutput, calls=%fused_computation.103 | convolution fusion | flops 50331648 | bytes 1130496 | tf_op jit(solution)/shard_map/dot_general | solution.py:39
  62.8 2.0 fusion.38
  64.8 0.6 fusion.78
  65.4 1.3 collective-permute-start.6
  66.7 4.3 %fusion.6 = f32[16,1024]{1,0:T(8,128)S(1)} fusion(f32[16,1024]{1,0:T(8,128)S(1)} %fusion.38, f32[1536,1024]{1,0:T(8,128)} %copy-done), kind=kOutput, calls=%fused_computation.43 | convolution fusion | flops 201326592 | bytes 4325376 | tf_op jit(solution)/shard_map/dot_general | solution.py:39
  71.0 1.5 collective-permute-start.7
  72.5 0.6 convolution_add_fusion.7
  73.1 1.8 collective-permute-done.7
  75.0 0.6 fusion.41
  75.6 0.6 fusion.79
  76.2 4.4 %collective-permute-start.8 = (f32[16,256]{1,0:T(8,128)S(1)}, f32[16,256]{1,0:T(8,128)S(1)}, u32[]{:S(2)}, u32[]{:S(2)}) collective-permute-start(f32[16,256]{1,0:T(8,128)S(1)} %get-tuple-element.59), channel_id=1, source_target_pairs={{0,1},{1,2},{2,3},{3,4},{4,5},{5,6},{6,7},{7,8},{8,9},{9,10},{10,1... | collective-permute-start | bytes 49160 | tf_op jit(solution)/shard_map/ppermute | solution.py:72
  80.6 2.1 %fusion.4 = f32[16,1024]{1,0:T(8,128)S(1)} fusion(f32[16,1024]{1,0:T(8,128)S(1)} %fusion.41, f32[1536,1024]{1,0:T(8,128)S(1)} %copy-done.1), kind=kOutput, calls=%fused_computation.41 | convolution fusion | flops 201326592 | bytes 4325376 | tf_op jit(solution)/shard_map/dot_general | solution.py:39
  82.7 1.3 collective-permute-start.9
  84.0 0.6 convolution_add_fusion.5
  84.6 1.2 collective-permute-done.9
  85.8 0.6 fusion.44
  86.4 0.6 fusion.80
  87.0 5.9 %collective-permute-start.10 = (f32[16,256]{1,0:T(8,128)S(1)}, f32[16,256]{1,0:T(8,128)S(1)}, u32[]{:S(2)}, u32[]{:S(2)}) collective-permute-start(f32[16,256]{1,0:T(8,128)S(1)} %get-tuple-element.57), channel_id=1, source_target_pairs={{0,1},{1,2},{2,3},{3,4},{4,5},{5,6},{6,7},{7,8},{8,9},{9,10},{10,1... | collective-permute-start | bytes 49160 | tf_op jit(solution)/shard_map/ppermute | solution.py:72
  92.9 2.1 %fusion.2 = f32[16,1024]{1,0:T(8,128)S(1)} fusion(f32[16,1024]{1,0:T(8,128)S(1)} %fusion.44, f32[1536,1024]{1,0:T(8,128)S(1)} %copy-done.1), kind=kOutput, calls=%fused_computation.39 | convolution fusion | flops 201326592 | bytes 4325376 | tf_op jit(solution)/shard_map/dot_general | solution.py:39
  95.0 1.3 collective-permute-start.11
  96.9 1.2 collective-permute-done.11
  98.1 0.6 fusion.47
  98.7 0.6 fusion.81
  99.4 4.8 %collective-permute-start.12 = (f32[16,256]{1,0:T(8,128)S(1)}, f32[16,256]{1,0:T(8,128)S(1)}, u32[]{:S(2)}, u32[]{:S(2)}) collective-permute-start(f32[16,256]{1,0:T(8,128)S(1)} %get-tuple-element.55), channel_id=1, source_target_pairs={{0,1},{1,2},{2,3},{3,4},{4,5},{5,6},{6,7},{7,8},{8,9},{9,10},{10,1... | collective-permute-start | bytes 49160 | tf_op jit(solution)/shard_map/ppermute | solution.py:72
  104.2 2.1 %fusion = f32[16,1024]{1,0:T(8,128)S(1)} fusion(f32[16,1024]{1,0:T(8,128)S(1)} %fusion.47, f32[1536,1024]{1,0:T(8,128)S(1)} %copy-done.1), kind=kOutput, calls=%fused_computation.37 | convolution fusion | flops 201326592 | bytes 4325376 | tf_op jit(solution)/shard_map/dot_general | solution.py:39
  106.3 1.5 collective-permute-start.13
  108.4 0.9 collective-permute-done.13
  109.3 0.6 fusion.23
  110.0 7.3 %collective-permute-start.14 = (f32[2,16,1024]{2,1,0:T(8,128)S(1)}, f32[2,16,1024]{2,1,0:T(8,128)S(1)}, u32[]{:S(2)}, u32[]{:S(2)}) collective-permute-start(f32[2,16,1024]{2,1,0:T(8,128)S(1)} %pad_maximum_fusion.3), channel_id=1, source_target_pairs={{0,128},{16,144},{32,160},{48,176},{64,192},{80,208},{96,224},{112... | collective-permute-start | bytes 393224 | tf_op jit(solution)/shard_map/ppermute | solution.py:111
  117.3 3.4 %collective-permute-done.14 = f32[2,16,1024]{2,1,0:T(8,128)S(1)} collective-permute-done((f32[2,16,1024]{2,1,0:T(8,128)S(1)}, f32[2,16,1024]{2,1,0:T(8,128)S(1)}, u32[]{:S(2)}, u32[]{:S(2)}) %collective-permute-start.14) | collective-permute-done | bytes 131104 | tf_op jit(solution)/shard_map/ppermute | solution.py:111
  120.7 5.5 %collective-permute-start.15 = (f32[2,2,16,1024]{3,2,1,0:T(8,128)S(1)}, f32[2,2,16,1024]{3,2,1,0:T(8,128)S(1)}, u32[]{:S(2)}, u32[]{:S(2)}) collective-permute-start(f32[2,2,16,1024]{3,2,1,0:T(8,128)S(1)} %pad_maximum_fusion.2), channel_id=1, source_target_pairs={{0,64},{16,80},{32,96},{48,112},{64,0},{80,16},{96,32},{112,48},{1... | collective-permute-start | bytes 786440 | tf_op jit(solution)/shard_map/ppermute | solution.py:111
  126.2 11.4 %collective-permute-done.15 = f32[2,2,16,1024]{3,2,1,0:T(8,128)S(1)} collective-permute-done((f32[2,2,16,1024]{3,2,1,0:T(8,128)S(1)}, f32[2,2,16,1024]{3,2,1,0:T(8,128)S(1)}, u32[]{:S(2)}, u32[]{:S(2)}) %collective-permute-start.15) | collective-permute-done | bytes 262176 | tf_op jit(solution)/shard_map/ppermute | solution.py:111
  138.3 14.9 %collective-permute-done.16 = f32[2,2,2,16,1024]{4,3,2,1,0:T(8,128)S(1)} collective-permute-done((f32[2,2,2,16,1024]{4,3,2,1,0:T(8,128)S(1)}, f32[2,2,2,16,1024]{4,3,2,1,0:T(8,128)S(1)}, u32[]{:S(2)}, u32[]{:S(2)}) %collective-permute-start.16) | collective-permute-done | bytes 524320 | tf_op jit(solution)/shard_map/ppermute | solution.py:111
  153.6 24.3 %collective-permute-done.17 = f32[2,2,2,2,16,1024]{5,4,3,2,1,0:T(8,128)S(1)} collective-permute-done((f32[2,2,2,2,16,1024]{5,4,3,2,1,0:T(8,128)S(1)}, f32[2,2,2,2,16,1024]{5,4,3,2,1,0:T(8,128)S(1)}, u32[]{:S(2)}, u32[]{:S(2)}) %collective-permute-start.17) | collective-permute-done | bytes 1048608 | tf_op jit(solution)/shard_map/ppermute | solution.py:111
  178.1 1.8 fusion.14
  180.3 1.2 collective-permute-done.18
  181.6 2.1 %collective-permute-start.19 = (f32[32,1,2,2,16]{0,4,3,2,1:T(8,128)S(1)}, f32[32,1,2,2,16]{0,4,3,2,1:T(8,128)S(1)}, u32[]{:S(2)}, u32[]{:S(2)}) collective-permute-start(f32[32,1,2,2,16]{0,4,3,2,1:T(8,128)S(1)} %select_bitcast_fusion.9), channel_id=1, source_target_pairs={{0,2},{1,3},{2,0},{3,1},{4,6},{5,7},{6,4},{7,5},{8,10},{9,11},{10,... | collective-permute-start | bytes 24584 | tf_op jit(solution)/shard_map/ppermute | solution.py:111
  183.6 1.9 collective-permute-done.19
  185.6 2.2 %collective-permute-start.20 = (f32[32,1,1,2,16]{0,4,3,2,1:T(8,128)S(1)}, f32[32,1,1,2,16]{0,4,3,2,1:T(8,128)S(1)}, u32[]{:S(2)}, u32[]{:S(2)}) collective-permute-start(f32[32,1,1,2,16]{0,4,3,2,1:T(8,128)S(1)} %select_bitcast_fusion.10), channel_id=1, source_target_pairs={{0,4},{1,5},{2,6},{3,7},{4,0},{5,1},{6,2},{7,3},{8,12},{9,13},{10,... | collective-permute-start | bytes 12296 | tf_op jit(solution)/shard_map/ppermute | solution.py:111
  187.8 1.7 collective-permute-done.20
  189.6 2.8 %collective-permute-start.21 = (f32[32,1,1,1,16]{0,4,3,2,1:T(8,128)S(1)}, f32[32,1,1,1,16]{0,4,3,2,1:T(8,128)S(1)}, u32[]{:S(2)}, u32[]{:S(2)}) collective-permute-start(f32[32,1,1,1,16]{0,4,3,2,1:T(8,128)S(1)} %select_bitcast_fusion.11), channel_id=1, source_target_pairs={{0,8},{1,9},{2,10},{3,11},{4,12},{5,13},{6,14},{7,15},{8,0},{9,1},... | collective-permute-start | bytes 6152 | tf_op jit(solution)/shard_map/ppermute | solution.py:111
  192.4 2.4 %collective-permute-done.21 = f32[32,1,1,1,16]{0,4,3,2,1:T(8,128)S(1)} collective-permute-done((f32[32,1,1,1,16]{0,4,3,2,1:T(8,128)S(1)}, f32[32,1,1,1,16]{0,4,3,2,1:T(8,128)S(1)}, u32[]{:S(2)}, u32[]{:S(2)}) %collective-permute-start.21) | collective-permute-done | bytes 2080 | tf_op jit(solution)/shard_map/ppermute | solution.py:111
  194.9 0.7 copy.10
  195.6 0.7 copy.9
  (52 shorter events, 4.2 us)
Async XLA Ops:
  0.6 39.5 %copy-start.3 = (f32[16,1024]{1,0:T(8,128)S(1)}, f32[16,1024]{1,0:T(8,128)}, u32[]{:S(2)}) copy-start(f32[16,1024]{1,0:T(8,128)} %param.5) | copy-start | bytes 196612
  3.3 39.1 %collective-permute-start = (f32[2]{0:T(128)S(1)}, f32[2]{0:T(128)S(1)}, u32[]{:S(2)}, u32[]{:S(2)}) collective-permute-start(f32[2]{0:T(128)S(1)} %pad_maximum_fusion.4), channel_id=1, source_target_pairs={{0,1},{1,0},{2,3},{3,2},{4,5},{5,4},{6,7},{7,6},{8,9},{9,8},{10,11... | collective-permute-start | bytes 32 | tf_op jit(solution)/shard_map/ppermute | solution.py:111
  6.8 56.0 %copy-start.4 = (f32[1024]{0:T(1024)S(1)}, f32[1024]{0:T(1024)}, u32[]{:S(2)}) copy-start(f32[1024]{0:T(1024)} %param.6) | copy-start | bytes 12292
  6.8 56.0 %collective-permute-start.4 = (f32[16,256]{1,0:T(8,128)S(1)}, f32[16,256]{1,0:T(8,128)S(1)}, u32[]{:S(2)}, u32[]{:S(2)}) collective-permute-start(f32[16,256]{1,0:T(8,128)S(1)} %get-tuple-element.62), channel_id=1, source_target_pairs={{0,1},{1,2},{2,3},{3,4},{4,5},{5,6},{6,7},{7,8},{8,9},{9,10},{10,1... | collective-permute-start | bytes 49160 | tf_op jit(solution)/shard_map/ppermute | solution.py:72
  9.3 51.6 %collective-permute-start.5 = (f32[16,256]{1,0:T(8,128)S(1)}, f32[16,256]{1,0:T(8,128)S(1)}, u32[]{:S(2)}, u32[]{:S(2)}) collective-permute-start(f32[16,256]{1,0:T(8,128)S(1)} %get-tuple-element.63), channel_id=1, source_target_pairs={{1,0},{2,1},{3,2},{4,3},{5,4},{6,5},{7,6},{8,7},{9,8},{10,9},{11,1... | collective-permute-start | bytes 49160 | tf_op jit(solution)/shard_map/ppermute | solution.py:73
  37.5 2.6 %copy-start = (f32[1536,1024]{1,0:T(8,128)}, f32[1536,1024]{1,0:T(8,128)S(1)}, u32[]{:S(2)}) copy-start(f32[1536,1024]{1,0:T(8,128)S(1)} %multiply_add_fusion) | copy-start | bytes 18874372
  43.1 4.6 %collective-permute-start.1 = (f32[2]{0:T(128)S(1)}, f32[2]{0:T(128)S(1)}, u32[]{:S(2)}, u32[]{:S(2)}) collective-permute-start(f32[2]{0:T(128)S(1)} %fusion.107), channel_id=1, source_target_pairs={{0,2},{1,3},{2,0},{3,1},{4,6},{5,7},{6,4},{7,5},{8,10},{9,11},{10,... | collective-permute-start | bytes 32 | tf_op jit(solution)/shard_map/ppermute | solution.py:111
  48.5 4.9 %collective-permute-start.2 = (f32[2]{0:T(128)S(1)}, f32[2]{0:T(128)S(1)}, u32[]{:S(2)}, u32[]{:S(2)}) collective-permute-start(f32[2]{0:T(128)S(1)} %fusion.108), channel_id=1, source_target_pairs={{0,4},{1,5},{2,6},{3,7},{4,0},{5,1},{6,2},{7,3},{8,12},{9,13},{10,... | collective-permute-start | bytes 32 | tf_op jit(solution)/shard_map/ppermute | solution.py:111
  53.4 5.2 %collective-permute-start.3 = (f32[2]{0:T(128)S(1)}, f32[2]{0:T(128)S(1)}, u32[]{:S(2)}, u32[]{:S(2)}) collective-permute-start(f32[2]{0:T(128)S(1)} %max.14), channel_id=1, source_target_pairs={{0,8},{1,9},{2,10},{3,11},{4,12},{5,13},{6,14},{7,15},{8,0},{9,1},... | collective-permute-start | bytes 32 | tf_op jit(solution)/shard_map/ppermute | solution.py:111
  60.8 11.7 %copy-start.1 = (f32[1536,1024]{1,0:T(8,128)S(1)}, f32[1536,1024]{1,0:T(8,128)}, u32[]{:S(2)}) copy-start(f32[1536,1024]{1,0:T(8,128)} %copy-done) | copy-start | bytes 18874372
  65.4 7.1 %collective-permute-start.6 = (f32[16,256]{1,0:T(8,128)S(1)}, f32[16,256]{1,0:T(8,128)S(1)}, u32[]{:S(2)}, u32[]{:S(2)}) collective-permute-start(f32[16,256]{1,0:T(8,128)S(1)} %get-tuple-element.61), channel_id=1, source_target_pairs={{0,1},{1,2},{2,3},{3,4},{4,5},{5,6},{6,7},{7,8},{8,9},{9,10},{10,1... | collective-permute-start | bytes 49160 | tf_op jit(solution)/shard_map/ppermute | solution.py:72
  71.0 3.9 %collective-permute-start.7 = (f32[16,256]{1,0:T(8,128)S(1)}, f32[16,256]{1,0:T(8,128)S(1)}, u32[]{:S(2)}, u32[]{:S(2)}) collective-permute-start(f32[16,256]{1,0:T(8,128)S(1)} %get-tuple-element.60), channel_id=1, source_target_pairs={{1,0},{2,1},{3,2},{4,3},{5,4},{6,5},{7,6},{8,7},{9,8},{10,9},{11,1... | collective-permute-start | bytes 49160 | tf_op jit(solution)/shard_map/ppermute | solution.py:73
  76.2 7.8 %collective-permute-start.8 = (f32[16,256]{1,0:T(8,128)S(1)}, f32[16,256]{1,0:T(8,128)S(1)}, u32[]{:S(2)}, u32[]{:S(2)}) collective-permute-start(f32[16,256]{1,0:T(8,128)S(1)} %get-tuple-element.59), channel_id=1, source_target_pairs={{0,1},{1,2},{2,3},{3,4},{4,5},{5,6},{6,7},{7,8},{8,9},{9,10},{10,1... | collective-permute-start | bytes 49160 | tf_op jit(solution)/shard_map/ppermute | solution.py:72
  82.7 3.1 %collective-permute-start.9 = (f32[16,256]{1,0:T(8,128)S(1)}, f32[16,256]{1,0:T(8,128)S(1)}, u32[]{:S(2)}, u32[]{:S(2)}) collective-permute-start(f32[16,256]{1,0:T(8,128)S(1)} %get-tuple-element.58), channel_id=1, source_target_pairs={{1,0},{2,1},{3,2},{4,3},{5,4},{6,5},{7,6},{8,7},{9,8},{10,9},{11,1... | collective-permute-start | bytes 49160 | tf_op jit(solution)/shard_map/ppermute | solution.py:73
  87.0 9.3 %collective-permute-start.10 = (f32[16,256]{1,0:T(8,128)S(1)}, f32[16,256]{1,0:T(8,128)S(1)}, u32[]{:S(2)}, u32[]{:S(2)}) collective-permute-start(f32[16,256]{1,0:T(8,128)S(1)} %get-tuple-element.57), channel_id=1, source_target_pairs={{0,1},{1,2},{2,3},{3,4},{4,5},{5,6},{6,7},{7,8},{8,9},{9,10},{10,1... | collective-permute-start | bytes 49160 | tf_op jit(solution)/shard_map/ppermute | solution.py:72
  95.0 3.1 %collective-permute-start.11 = (f32[16,256]{1,0:T(8,128)S(1)}, f32[16,256]{1,0:T(8,128)S(1)}, u32[]{:S(2)}, u32[]{:S(2)}) collective-permute-start(f32[16,256]{1,0:T(8,128)S(1)} %get-tuple-element.56), channel_id=1, source_target_pairs={{1,0},{2,1},{3,2},{4,3},{5,4},{6,5},{7,6},{8,7},{9,8},{10,9},{11,1... | collective-permute-start | bytes 49160 | tf_op jit(solution)/shard_map/ppermute | solution.py:73
  98.7 79.4 %copy-start.2 = (f32[16,1024]{1,0:T(8,128)}, f32[16,1024]{1,0:T(8,128)S(1)}, u32[]{:S(2)}) copy-start(f32[16,1024]{1,0:T(8,128)S(1)} %fusion.47) | copy-start | bytes 196612
  99.4 8.4 %collective-permute-start.12 = (f32[16,256]{1,0:T(8,128)S(1)}, f32[16,256]{1,0:T(8,128)S(1)}, u32[]{:S(2)}, u32[]{:S(2)}) collective-permute-start(f32[16,256]{1,0:T(8,128)S(1)} %get-tuple-element.55), channel_id=1, source_target_pairs={{0,1},{1,2},{2,3},{3,4},{4,5},{5,6},{6,7},{7,8},{8,9},{9,10},{10,1... | collective-permute-start | bytes 49160 | tf_op jit(solution)/shard_map/ppermute | solution.py:72
  106.3 3.1 %collective-permute-start.13 = (f32[16,256]{1,0:T(8,128)S(1)}, f32[16,256]{1,0:T(8,128)S(1)}, u32[]{:S(2)}, u32[]{:S(2)}) collective-permute-start(f32[16,256]{1,0:T(8,128)S(1)} %get-tuple-element.54), channel_id=1, source_target_pairs={{1,0},{2,1},{3,2},{4,3},{5,4},{6,5},{7,6},{8,7},{9,8},{10,9},{11,1... | collective-permute-start | bytes 49160 | tf_op jit(solution)/shard_map/ppermute | solution.py:73
  110.0 10.7 %collective-permute-start.14 = (f32[2,16,1024]{2,1,0:T(8,128)S(1)}, f32[2,16,1024]{2,1,0:T(8,128)S(1)}, u32[]{:S(2)}, u32[]{:S(2)}) collective-permute-start(f32[2,16,1024]{2,1,0:T(8,128)S(1)} %pad_maximum_fusion.3), channel_id=1, source_target_pairs={{0,128},{16,144},{32,160},{48,176},{64,192},{80,208},{96,224},{112... | collective-permute-start | bytes 393224 | tf_op jit(solution)/shard_map/ppermute | solution.py:111
  120.7 16.9 %collective-permute-start.15 = (f32[2,2,16,1024]{3,2,1,0:T(8,128)S(1)}, f32[2,2,16,1024]{3,2,1,0:T(8,128)S(1)}, u32[]{:S(2)}, u32[]{:S(2)}) collective-permute-start(f32[2,2,16,1024]{3,2,1,0:T(8,128)S(1)} %pad_maximum_fusion.2), channel_id=1, source_target_pairs={{0,64},{16,80},{32,96},{48,112},{64,0},{80,16},{96,32},{112,48},{1... | collective-permute-start | bytes 786440 | tf_op jit(solution)/shard_map/ppermute | solution.py:111
  137.7 15.5 %collective-permute-start.16 = (f32[2,2,2,16,1024]{4,3,2,1,0:T(8,128)S(1)}, f32[2,2,2,16,1024]{4,3,2,1,0:T(8,128)S(1)}, u32[]{:S(2)}, u32[]{:S(2)}) collective-permute-start(f32[2,2,2,16,1024]{4,3,2,1,0:T(8,128)S(1)} %pad_maximum_fusion.1), channel_id=1, source_target_pairs={{0,16},{16,0},{32,48},{48,32},{64,80},{80,64},{96,112},{112,96},{1... | collective-permute-start | bytes 1572872 | tf_op jit(solution)/shard_map/ppermute | solution.py:111
  153.5 24.4 %collective-permute-start.17 = (f32[2,2,2,2,16,1024]{5,4,3,2,1,0:T(8,128)S(1)}, f32[2,2,2,2,16,1024]{5,4,3,2,1,0:T(8,128)S(1)}, u32[]{:S(2)}, u32[]{:S(2)}) collective-permute-start(f32[2,2,2,2,16,1024]{5,4,3,2,1,0:T(8,128)S(1)} %pad_maximum_fusion), channel_id=1, source_target_pairs={{0,32},{16,48},{32,0},{48,16},{64,96},{80,112},{96,64},{112,80},{1... | collective-permute-start | bytes 3145736 | tf_op jit(solution)/shard_map/ppermute | solution.py:111
  180.2 1.3 collective-permute-start.18
  181.6 4.0 %collective-permute-start.19 = (f32[32,1,2,2,16]{0,4,3,2,1:T(8,128)S(1)}, f32[32,1,2,2,16]{0,4,3,2,1:T(8,128)S(1)}, u32[]{:S(2)}, u32[]{:S(2)}) collective-permute-start(f32[32,1,2,2,16]{0,4,3,2,1:T(8,128)S(1)} %select_bitcast_fusion.9), channel_id=1, source_target_pairs={{0,2},{1,3},{2,0},{3,1},{4,6},{5,7},{6,4},{7,5},{8,10},{9,11},{10,... | collective-permute-start | bytes 24584 | tf_op jit(solution)/shard_map/ppermute | solution.py:111
  185.6 3.9 %collective-permute-start.20 = (f32[32,1,1,2,16]{0,4,3,2,1:T(8,128)S(1)}, f32[32,1,1,2,16]{0,4,3,2,1:T(8,128)S(1)}, u32[]{:S(2)}, u32[]{:S(2)}) collective-permute-start(f32[32,1,1,2,16]{0,4,3,2,1:T(8,128)S(1)} %select_bitcast_fusion.10), channel_id=1, source_target_pairs={{0,4},{1,5},{2,6},{3,7},{4,0},{5,1},{6,2},{7,3},{8,12},{9,13},{10,... | collective-permute-start | bytes 12296 | tf_op jit(solution)/shard_map/ppermute | solution.py:111
  189.6 5.2 %collective-permute-start.21 = (f32[32,1,1,1,16]{0,4,3,2,1:T(8,128)S(1)}, f32[32,1,1,1,16]{0,4,3,2,1:T(8,128)S(1)}, u32[]{:S(2)}, u32[]{:S(2)}) collective-permute-start(f32[32,1,1,1,16]{0,4,3,2,1:T(8,128)S(1)} %select_bitcast_fusion.11), channel_id=1, source_target_pairs={{0,8},{1,9},{2,10},{3,11},{4,12},{5,13},{6,14},{7,15},{8,0},{9,1},... | collective-permute-start | bytes 6152 | tf_op jit(solution)/shard_map/ppermute | solution.py:111

commit v3 on v2

--- a/solution.py
+++ b/solution.py
@@ -167,18 +167,21 @@
 
     filtered = filter_block(orbitals, operator_fn, lowest, highest)
     applied = operator_fn(filtered)
+    band_steps = (8, 4, 1, 2)
+    gathered = gather_blocks(filtered, "band", band_steps)
     both = jnp.stack([filtered, applied])
-    band_steps = (8, 4, 1, 2)
-    gathered = gather_blocks(both, "band", band_steps)
     parts = jnp.einsum(
-        "rq,abcdsjq->srdcabj",
-        filtered,
+        "srq,abcdjq->srdcabj",
+        both,
         gathered,
         precision=lax.Precision.HIGHEST,
         preferred_element_type=jnp.float32,
     )
     parts = jnp.transpose(parts, (0, 1, 5, 4, 3, 2, 6)).reshape(2 * rows, 2, 2, 2, 2, rows)
     sums = scatter_sum(parts, "domain", (1, 2, 4, 8)).reshape(2, rows, rows)
+    swap = [(b * domain_count + d, d * domain_count + b) for b in range(band_count) for d in range(domain_count)]
+    mirrored = lax.ppermute(sums[1], ("band", "domain"), swap)
+    sums = jnp.stack([sums[0], mirrored.T])
     return (filtered, sums[0] / total_points, sums[1] / total_points)
 
 

time: 198 us -> 174 us (0.88)
  the two profiles are of different devices: /device:TPU:4 before, /device:TPU:20 now
where the time goes in v3:
time: 174 us; the launch traced here: 173 us
  starting transfers between devices  52 us (30%)
  waiting for transfers between devices  48.9 us (28%)
  matrix products  31.3 us (18%)
  other arithmetic  29.8 us (17%)
  local copies, waits for them, and re-layouts  7.76 us (4%)
  between operations  3.39 us (2%)
    ppermute x12, waiting for transfers between devices, exchange(): return lax.ppermute(value, axis, [(i, i ^ step) for i in range(count)])  38.1 us
    dot_general x20, matrix products, dense(): lax.dot_general(left, right, (((1,), (0,)), ((), ())), precision=lax.Prec...  30.3 us
    add x1, other arithmetic, stencil_matrix(): total = total + WEIGHTS[distance + 1] * count  24.2 us
    ppermute x5, starting transfers between devices, apply_operator(): from_above = lax.ppermute(outgoing[:, :capacity], 'domain', backward)  20.4 us
    ppermute x12, starting transfers between devices, exchange(): return lax.ppermute(value, axis, [(i, i ^ step) for i in range(count)])  16.8 us
    ppermute x5, starting transfers between devices, apply_operator(): from_below = lax.ppermute(outgoing[:, capacity:], 'domain', forward)  10.4 us
    ppermute x1, waiting for transfers between devices, shards(): mirrored = lax.ppermute(sums[1], ('band', 'domain'), swap)  8.6 us
    ppermute x1, starting transfers between devices, shards(): mirrored = lax.ppermute(sums[1], ('band', 'domain'), swap)  4.4 us
  transfers between devices with their start and end apart: 23, of which 15 were waited for; matrix products, arithmetic and copies ran while one was open for 33% of the time, Pallas kernels for 0%

profile of v3, /device:TPU:20, one launch (start us, length us, event | category | flops | bytes accessed | tf_op | source)
XLA Modules:
  0.0 173.1 jit_solution(14969821372410626698)
XLA Ops:
  0.6 1.3 fusion.62
  2.6 0.7 pad_maximum_fusion.3
  3.4 0.7 iota_compare_fusion.38
  4.1 0.8 fusion.70
  5.4 1.5 convolution_bitcast_fusion.1
  6.8 2.4 %collective-permute-start.4 = (f32[16,256]{1,0:T(8,128)S(1)}, f32[16,256]{1,0:T(8,128)S(1)}, u32[]{:S(2)}, u32[]{:S(2)}) collective-permute-start(f32[16,256]{1,0:T(8,128)S(1)} %get-tuple-element.59), channel_id=1, source_target_pairs={{0,1},{1,2},{2,3},{3,4},{4,5},{5,6},{6,7},{7,8},{8,9},{9,10},{10,1... | collective-permute-start | bytes 49160 | tf_op jit(solution)/shard_map/ppermute | solution.py:72
  9.3 4.1 %collective-permute-start.5 = (f32[16,256]{1,0:T(8,128)S(1)}, f32[16,256]{1,0:T(8,128)S(1)}, u32[]{:S(2)}, u32[]{:S(2)}) collective-permute-start(f32[16,256]{1,0:T(8,128)S(1)} %get-tuple-element.60), channel_id=1, source_target_pairs={{1,0},{2,1},{3,2},{4,3},{5,4},{6,5},{7,6},{8,7},{9,8},{10,9},{11,1... | collective-permute-start | bytes 49160 | tf_op jit(solution)/shard_map/ppermute | solution.py:73
  13.3 1.3 fusion.64
  14.7 1.4 fusion.63
  16.0 24.2 %multiply_add_fusion = f32[1536,1024]{1,0:T(8,128)S(1)} fusion(s32[1024]{0:T(1024)S(1)} %bitcast.154, s32[1024]{0:T(1024)S(1)} %bitcast.155, s32[1024]{0:T(1024)S(1)} %bitcast.157, s32[1024]{0:T(1024)S(1)} %bitcast.158, s32[1024]{0:T(1024)S(1)} %bitcast.159, s32[1024]{0:T(1024)S(1)} %bitcast.160, s32[1024]{0:T(1024)S(1)} %bitcast.161, s32[1024]{0:T(1024)S(1)} %bitcast.162, ...), kind=kLoop, calls=%fused_computation | loop fusion | flops 177733632 | bytes 6438912 | tf_op jit(solution)/shard_map/add | solution.py:55
  40.3 2.6 %copy-done = f32[1536,1024]{1,0:T(8,128)} copy-done((f32[1536,1024]{1,0:T(8,128)}, f32[1536,1024]{1,0:T(8,128)S(1)}, u32[]{:S(2)}) %copy-start) | copy-done | bytes 6291480
  42.9 2.3 %fusion.10 = f32[16,1024]{1,0:T(8,128)S(1)} fusion(f32[16,1024]{1,0:T(8,128)S(1)} %copy-done.3, f32[1536,1024]{1,0:T(8,128)S(1)} %multiply_add_fusion), kind=kOutput, calls=%fused_computation.49 | convolution fusion | flops 201326592 | bytes 4325376 | tf_op jit(solution)/shard_map/dot_general | solution.py:39
  45.2 0.7 fusion.101
  46.2 3.3 %collective-permute-done.1 = f32[2]{0:T(128)S(1)} collective-permute-done((f32[2]{0:T(128)S(1)}, f32[2]{0:T(128)S(1)}, u32[]{:S(2)}, u32[]{:S(2)}) %collective-permute-start.1) | collective-permute-done | bytes 40 | tf_op jit(solution)/shard_map/ppermute | solution.py:111
  49.5 0.7 fusion.102
  50.2 1.3 collective-permute-start.2
  51.5 2.3 %collective-permute-done.2 = f32[2]{0:T(128)S(1)} collective-permute-done((f32[2]{0:T(128)S(1)}, f32[2]{0:T(128)S(1)}, u32[]{:S(2)}, u32[]{:S(2)}) %collective-permute-start.2) | collective-permute-done | bytes 40 | tf_op jit(solution)/shard_map/ppermute | solution.py:111
  53.8 5.1 %collective-permute-done.3 = f32[2]{0:T(128)S(1)} collective-permute-done((f32[2]{0:T(128)S(1)}, f32[2]{0:T(128)S(1)}, u32[]{:S(2)}, u32[]{:S(2)}) %collective-permute-start.3) | collective-permute-done | bytes 40 | tf_op jit(solution)/shard_map/ppermute | solution.py:111
  61.2 2.0 %fusion.49 = f32[16,1024]{1,0:T(8,128)S(1)} fusion(f32[16,256]{1,0:T(8,128)S(1)} %collective-permute-done.5, f32[1536,1024]{1,0:T(8,128)} %copy-done), kind=kOutput, calls=%fused_computation.99 | convolution fusion | flops 50331648 | bytes 1130496 | tf_op jit(solution)/shard_map/dot_general | solution.py:39
  63.2 2.0 %fusion.31 = f32[16,1024]{1,0:T(8,128)S(1)} fusion(f32[16,1024]{1,0:T(8,128)S(1)} %fusion.49, f32[16,1024]{1,0:T(8,128)S(1)} %fusion.10, f32[16,256]{1,0:T(8,128)S(1)} %collective-permute-done.4, f32[1536,1024]{1,0:T(8,128)} %copy-done, f32[16,1024]{1,0:T(8,128)S(1)} %copy-done.3, f32[]{:T(128)S(6)} %div.43, f32[]{:T(128)S(6)} %div.53, f32[1024]{0:T(1024)S(1)} %copy-done.4), kind=kOutput, calls=%fused_computation.77 | convolution fusion | flops 50495488 | bytes 1331208 | tf_op jit(solution)/shard_map/dot_general | solution.py:39
  65.1 0.6 fusion.72
  65.8 1.9 %collective-permute-start.6 = (f32[16,256]{1,0:T(8,128)S(1)}, f32[16,256]{1,0:T(8,128)S(1)}, u32[]{:S(2)}, u32[]{:S(2)}) collective-permute-start(f32[16,256]{1,0:T(8,128)S(1)} %get-tuple-element.58), channel_id=1, source_target_pairs={{0,1},{1,2},{2,3},{3,4},{4,5},{5,6},{6,7},{7,8},{8,9},{9,10},{10,1... | collective-permute-start | bytes 49160 | tf_op jit(solution)/shard_map/ppermute | solution.py:72
  67.7 4.3 %fusion.6 = f32[16,1024]{1,0:T(8,128)S(1)} fusion(f32[16,1024]{1,0:T(8,128)S(1)} %fusion.31, f32[1536,1024]{1,0:T(8,128)} %copy-done), kind=kOutput, calls=%fused_computation.43 | convolution fusion | flops 201326592 | bytes 4325376 | tf_op jit(solution)/shard_map/dot_general | solution.py:39
  72.0 4.7 %collective-permute-start.7 = (f32[16,256]{1,0:T(8,128)S(1)}, f32[16,256]{1,0:T(8,128)S(1)}, u32[]{:S(2)}, u32[]{:S(2)}) collective-permute-start(f32[16,256]{1,0:T(8,128)S(1)} %get-tuple-element.57), channel_id=1, source_target_pairs={{1,0},{2,1},{3,2},{4,3},{5,4},{6,5},{7,6},{8,7},{9,8},{10,9},{11,1... | collective-permute-start | bytes 49160 | tf_op jit(solution)/shard_map/ppermute | solution.py:73
  76.7 0.6 convolution_add_fusion.7
  77.3 0.6 collective-permute-done.7
  77.9 0.6 fusion.34
  78.6 0.6 fusion.73
  79.2 1.9 %collective-permute-start.8 = (f32[16,256]{1,0:T(8,128)S(1)}, f32[16,256]{1,0:T(8,128)S(1)}, u32[]{:S(2)}, u32[]{:S(2)}) collective-permute-start(f32[16,256]{1,0:T(8,128)S(1)} %get-tuple-element.56), channel_id=1, source_target_pairs={{0,1},{1,2},{2,3},{3,4},{4,5},{5,6},{6,7},{7,8},{8,9},{9,10},{10,1... | collective-permute-start | bytes 49160 | tf_op jit(solution)/shard_map/ppermute | solution.py:72
  81.1 2.1 %fusion.4 = f32[16,1024]{1,0:T(8,128)S(1)} fusion(f32[16,1024]{1,0:T(8,128)S(1)} %fusion.34, f32[1536,1024]{1,0:T(8,128)S(1)} %copy-done.1), kind=kOutput, calls=%fused_computation.41 | convolution fusion | flops 201326592 | bytes 4325376 | tf_op jit(solution)/shard_map/dot_general | solution.py:39
  83.2 4.5 %collective-permute-start.9 = (f32[16,256]{1,0:T(8,128)S(1)}, f32[16,256]{1,0:T(8,128)S(1)}, u32[]{:S(2)}, u32[]{:S(2)}) collective-permute-start(f32[16,256]{1,0:T(8,128)S(1)} %get-tuple-element.55), channel_id=1, source_target_pairs={{1,0},{2,1},{3,2},{4,3},{5,4},{6,5},{7,6},{8,7},{9,8},{10,9},{11,1... | collective-permute-start | bytes 49160 | tf_op jit(solution)/shard_map/ppermute | solution.py:73
  87.8 0.6 convolution_add_fusion.5
  88.4 0.8 collective-permute-done.9
  89.2 0.6 fusion.37
  89.8 0.6 fusion.74
  90.4 2.2 %collective-permute-start.10 = (f32[16,256]{1,0:T(8,128)S(1)}, f32[16,256]{1,0:T(8,128)S(1)}, u32[]{:S(2)}, u32[]{:S(2)}) collective-permute-start(f32[16,256]{1,0:T(8,128)S(1)} %get-tuple-element.54), channel_id=1, source_target_pairs={{0,1},{1,2},{2,3},{3,4},{4,5},{5,6},{6,7},{7,8},{8,9},{9,10},{10,1... | collective-permute-start | bytes 49160 | tf_op jit(solution)/shard_map/ppermute | solution.py:72
  92.7 2.1 %fusion.2 = f32[16,1024]{1,0:T(8,128)S(1)} fusion(f32[16,1024]{1,0:T(8,128)S(1)} %fusion.37, f32[1536,1024]{1,0:T(8,128)S(1)} %copy-done.1), kind=kOutput, calls=%fused_computation.39 | convolution fusion | flops 201326592 | bytes 4325376 | tf_op jit(solution)/shard_map/dot_general | solution.py:39
  94.7 4.2 %collective-permute-start.11 = (f32[16,256]{1,0:T(8,128)S(1)}, f32[16,256]{1,0:T(8,128)S(1)}, u32[]{:S(2)}, u32[]{:S(2)}) collective-permute-start(f32[16,256]{1,0:T(8,128)S(1)} %get-tuple-element.53), channel_id=1, source_target_pairs={{1,0},{2,1},{3,2},{4,3},{5,4},{6,5},{7,6},{8,7},{9,8},{10,9},{11,1... | collective-permute-start | bytes 49160 | tf_op jit(solution)/shard_map/ppermute | solution.py:73
  99.0 0.6 convolution_add_fusion.3
  99.6 0.8 collective-permute-done.11
  100.4 0.6 fusion.40
  101.1 7.3 %collective-permute-start.12 = (f32[16,1024]{1,0:T(8,128)S(1)}, f32[16,1024]{1,0:T(8,128)S(1)}, u32[]{:S(2)}, u32[]{:S(2)}) collective-permute-start(f32[16,1024]{1,0:T(8,128)S(1)} %fusion.40), channel_id=1, source_target_pairs={{0,128},{16,144},{32,160},{48,176},{64,192},{80,208},{96,224},{112... | collective-permute-start | bytes 196616 | tf_op jit(solution)/shard_map/ppermute | solution.py:111
  108.3 2.7 %collective-permute-done.12 = f32[16,1024]{1,0:T(8,128)S(1)} collective-permute-done((f32[16,1024]{1,0:T(8,128)S(1)}, f32[16,1024]{1,0:T(8,128)S(1)}, u32[]{:S(2)}, u32[]{:S(2)}) %collective-permute-start.12) | collective-permute-done | bytes 65568 | tf_op jit(solution)/shard_map/ppermute | solution.py:111
  111.0 3.3 %collective-permute-start.13 = (f32[2,16,1024]{2,1,0:T(8,128)S(1)}, f32[2,16,1024]{2,1,0:T(8,128)S(1)}, u32[]{:S(2)}, u32[]{:S(2)}) collective-permute-start(f32[2,16,1024]{2,1,0:T(8,128)S(1)} %pad_maximum_fusion.2), channel_id=1, source_target_pairs={{0,64},{16,80},{32,96},{48,112},{64,0},{80,16},{96,32},{112,48},{1... | collective-permute-start | bytes 393224 | tf_op jit(solution)/shard_map/ppermute | solution.py:111
  114.3 5.5 %collective-permute-done.13 = f32[2,16,1024]{2,1,0:T(8,128)S(1)} collective-permute-done((f32[2,16,1024]{2,1,0:T(8,128)S(1)}, f32[2,16,1024]{2,1,0:T(8,128)S(1)}, u32[]{:S(2)}, u32[]{:S(2)}) %collective-permute-start.13) | collective-permute-done | bytes 131104 | tf_op jit(solution)/shard_map/ppermute | solution.py:111
  120.5 0.6 fusion.75
  121.1 1.9 %collective-permute-start.16 = (f32[16,256]{1,0:T(8,128)S(1)}, f32[16,256]{1,0:T(8,128)S(1)}, u32[]{:S(2)}, u32[]{:S(2)}) collective-permute-start(f32[16,256]{1,0:T(8,128)S(1)} %get-tuple-element.52), channel_id=1, source_target_pairs={{0,1},{1,2},{2,3},{3,4},{4,5},{5,6},{6,7},{7,8},{8,9},{9,10},{10,1... | collective-permute-start | bytes 49160 | tf_op jit(solution)/shard_map/ppermute | solution.py:72
  123.0 6.4 %collective-permute-done.14 = f32[2,2,16,1024]{3,2,1,0:T(8,128)S(1)} collective-permute-done((f32[2,2,16,1024]{3,2,1,0:T(8,128)S(1)}, f32[2,2,16,1024]{3,2,1,0:T(8,128)S(1)}, u32[]{:S(2)}, u32[]{:S(2)}) %collective-permute-start.14) | collective-permute-done | bytes 262176 | tf_op jit(solution)/shard_map/ppermute | solution.py:111
  129.8 4.3 %fusion = f32[16,1024]{1,0:T(8,128)S(1)} fusion(f32[16,1024]{1,0:T(8,128)S(1)} %fusion.40, f32[1536,1024]{1,0:T(8,128)} %copy-done), kind=kOutput, calls=%fused_computation.37 | convolution fusion | flops 201326592 | bytes 4325376 | tf_op jit(solution)/shard_map/dot_general | solution.py:39
  134.1 2.9 %collective-permute-start.17 = (f32[16,256]{1,0:T(8,128)S(1)}, f32[16,256]{1,0:T(8,128)S(1)}, u32[]{:S(2)}, u32[]{:S(2)}) collective-permute-start(f32[16,256]{1,0:T(8,128)S(1)} %get-tuple-element.51), channel_id=1, source_target_pairs={{1,0},{2,1},{3,2},{4,3},{5,4},{6,5},{7,6},{8,7},{9,8},{10,9},{11,1... | collective-permute-start | bytes 49160 | tf_op jit(solution)/shard_map/ppermute | solution.py:73
  137.0 1.8 %convolution_add_fusion.1 = f32[16,1024]{1,0:T(8,128)S(1)} fusion(f32[16,1024]{1,0:T(8,128)S(1)} %fusion, f32[16,256]{1,0:T(8,128)S(1)} %collective-permute-done.16, f32[1536,1024]{1,0:T(8,128)} %copy-done), kind=kOutput, calls=%fused_computation.55 | convolution fusion | flops 50348032 | bytes 1196032 | tf_op jit(solution)/shard_map/dot_general | solution.py:39
  138.9 1.8 %fusion.16 = f32[1,16,1024]{2,1,0:T(8,128)S(1)} fusion(f32[16,1024]{1,0:T(8,128)S(1)} %convolution_add_fusion.1, f32[16,256]{1,0:T(8,128)S(1)} %collective-permute-done.17, f32[1536,1024]{1,0:T(8,128)} %copy-done, f32[16,1024]{1,0:T(8,128)S(1)} %fusion.40, f32[1024]{0:T(1024)S(1)} %copy-done.4), kind=kOutput, calls=%fused_computation.54 | convolution fusion | flops 50429952 | bytes 1265664 | tf_op jit(solution)/shard_map/dot_general | solution.py:39
  140.7 1.5 collective-permute-done.15
  142.3 1.0 convolution_bitcast_fusion
  143.7 1.2 collective-permute-done.18
  145.0 2.7 %collective-permute-start.19 = (f32[32,1,2,2,16]{0,4,3,2,1:T(8,128)S(1)}, f32[32,1,2,2,16]{0,4,3,2,1:T(8,128)S(1)}, u32[]{:S(2)}, u32[]{:S(2)}) collective-permute-start(f32[32,1,2,2,16]{0,4,3,2,1:T(8,128)S(1)} %select_bitcast_fusion.9), channel_id=1, source_target_pairs={{0,2},{1,3},{2,0},{3,1},{4,6},{5,7},{6,4},{7,5},{8,10},{9,11},{10,... | collective-permute-start | bytes 24584 | tf_op jit(solution)/shard_map/ppermute | solution.py:111
  147.8 1.9 %collective-permute-done.19 = f32[32,1,2,2,16]{0,4,3,2,1:T(8,128)S(1)} collective-permute-done((f32[32,1,2,2,16]{0,4,3,2,1:T(8,128)S(1)}, f32[32,1,2,2,16]{0,4,3,2,1:T(8,128)S(1)}, u32[]{:S(2)}, u32[]{:S(2)}) %collective-permute-start.19) | collective-permute-done | bytes 8224 | tf_op jit(solution)/shard_map/ppermute | solution.py:111
  149.8 3.7 %collective-permute-done.20 = f32[32,1,1,2,16]{0,4,3,2,1:T(8,128)S(1)} collective-permute-done((f32[32,1,1,2,16]{0,4,3,2,1:T(8,128)S(1)}, f32[32,1,1,2,16]{0,4,3,2,1:T(8,128)S(1)}, u32[]{:S(2)}, u32[]{:S(2)}) %collective-permute-start.20) | collective-permute-done | bytes 4128 | tf_op jit(solution)/shard_map/ppermute | solution.py:111
  153.5 0.7 collective-permute-start.21
  154.2 4.5 %collective-permute-done.21 = f32[32,1,1,1,16]{0,4,3,2,1:T(8,128)S(1)} collective-permute-done((f32[32,1,1,1,16]{0,4,3,2,1:T(8,128)S(1)}, f32[32,1,1,1,16]{0,4,3,2,1:T(8,128)S(1)}, u32[]{:S(2)}, u32[]{:S(2)}) %collective-permute-start.21) | collective-permute-done | bytes 2080 | tf_op jit(solution)/shard_map/ppermute | solution.py:111
  158.8 4.4 %collective-permute-start.22 = (f32[16,16]{0,1:T(8,128)S(1)}, f32[16,16]{0,1:T(8,128)S(1)}, u32[]{:S(2)}, u32[]{:S(2)}) collective-permute-start(f32[16,16]{0,1:T(8,128)S(1)} %get-tuple-element.61), channel_id=1, source_target_pairs={{0,0},{1,16},{2,32},{3,48},{4,64},{5,80},{6,96},{7,112},{8,128},{9... | collective-permute-start | bytes 3080 | tf_op jit(solution)/shard_map/ppermute | solution.py:183
  163.2 0.7 copy.9
  163.9 8.6 %collective-permute-done.22 = f32[16,16]{0,1:T(8,128)S(1)} collective-permute-done((f32[16,16]{0,1:T(8,128)S(1)}, f32[16,16]{0,1:T(8,128)S(1)}, u32[]{:S(2)}, u32[]{:S(2)}) %collective-permute-start.22) | collective-permute-done | bytes 1056 | tf_op jit(solution)/shard_map/ppermute | solution.py:183
  172.5 0.6 multiply_bitcast_fusion
  (53 shorter events, 3.3 us)
Async XLA Ops:
  0.6 42.2 %copy-start.3 = (f32[16,1024]{1,0:T(8,128)S(1)}, f32[16,1024]{1,0:T(8,128)}, u32[]{:S(2)}) copy-start(f32[16,1024]{1,0:T(8,128)} %param.5) | copy-start | bytes 196612
  3.3 41.8 %collective-permute-start = (f32[2]{0:T(128)S(1)}, f32[2]{0:T(128)S(1)}, u32[]{:S(2)}, u32[]{:S(2)}) collective-permute-start(f32[2]{0:T(128)S(1)} %pad_maximum_fusion.3), channel_id=1, source_target_pairs={{0,1},{1,0},{2,3},{3,2},{4,5},{5,4},{6,7},{7,6},{8,9},{9,8},{10,11... | collective-permute-start | bytes 32 | tf_op jit(solution)/shard_map/ppermute | solution.py:111
  6.8 56.4 %copy-start.4 = (f32[1024]{0:T(1024)S(1)}, f32[1024]{0:T(1024)}, u32[]{:S(2)}) copy-start(f32[1024]{0:T(1024)} %param.6) | copy-start | bytes 12292
  6.8 56.3 %collective-permute-start.4 = (f32[16,256]{1,0:T(8,128)S(1)}, f32[16,256]{1,0:T(8,128)S(1)}, u32[]{:S(2)}, u32[]{:S(2)}) collective-permute-start(f32[16,256]{1,0:T(8,128)S(1)} %get-tuple-element.59), channel_id=1, source_target_pairs={{0,1},{1,2},{2,3},{3,4},{4,5},{5,6},{6,7},{7,8},{8,9},{9,10},{10,1... | collective-permute-start | bytes 49160 | tf_op jit(solution)/shard_map/ppermute | solution.py:72
  9.3 51.9 %collective-permute-start.5 = (f32[16,256]{1,0:T(8,128)S(1)}, f32[16,256]{1,0:T(8,128)S(1)}, u32[]{:S(2)}, u32[]{:S(2)}) collective-permute-start(f32[16,256]{1,0:T(8,128)S(1)} %get-tuple-element.60), channel_id=1, source_target_pairs={{1,0},{2,1},{3,2},{4,3},{5,4},{6,5},{7,6},{8,7},{9,8},{10,9},{11,1... | collective-permute-start | bytes 49160 | tf_op jit(solution)/shard_map/ppermute | solution.py:73
  40.2 2.6 %copy-start = (f32[1536,1024]{1,0:T(8,128)}, f32[1536,1024]{1,0:T(8,128)S(1)}, u32[]{:S(2)}) copy-start(f32[1536,1024]{1,0:T(8,128)S(1)} %multiply_add_fusion) | copy-start | bytes 18874372
  45.9 3.6 %collective-permute-start.1 = (f32[2]{0:T(128)S(1)}, f32[2]{0:T(128)S(1)}, u32[]{:S(2)}, u32[]{:S(2)}) collective-permute-start(f32[2]{0:T(128)S(1)} %fusion.101), channel_id=1, source_target_pairs={{0,2},{1,3},{2,0},{3,1},{4,6},{5,7},{6,4},{7,5},{8,10},{9,11},{10,... | collective-permute-start | bytes 32 | tf_op jit(solution)/shard_map/ppermute | solution.py:111
  50.2 3.6 %collective-permute-start.2 = (f32[2]{0:T(128)S(1)}, f32[2]{0:T(128)S(1)}, u32[]{:S(2)}, u32[]{:S(2)}) collective-permute-start(f32[2]{0:T(128)S(1)} %fusion.102), channel_id=1, source_target_pairs={{0,4},{1,5},{2,6},{3,7},{4,0},{5,1},{6,2},{7,3},{8,12},{9,13},{10,... | collective-permute-start | bytes 32 | tf_op jit(solution)/shard_map/ppermute | solution.py:111
  53.8 5.1 %collective-permute-start.3 = (f32[2]{0:T(128)S(1)}, f32[2]{0:T(128)S(1)}, u32[]{:S(2)}, u32[]{:S(2)}) collective-permute-start(f32[2]{0:T(128)S(1)} %max.14), channel_id=1, source_target_pairs={{0,8},{1,9},{2,10},{3,11},{4,12},{5,13},{6,14},{7,15},{8,0},{9,1},... | collective-permute-start | bytes 32 | tf_op jit(solution)/shard_map/ppermute | solution.py:111
  61.2 15.6 %copy-start.1 = (f32[1536,1024]{1,0:T(8,128)S(1)}, f32[1536,1024]{1,0:T(8,128)}, u32[]{:S(2)}) copy-start(f32[1536,1024]{1,0:T(8,128)} %copy-done) | copy-start | bytes 18874372
  65.8 10.9 %collective-permute-start.6 = (f32[16,256]{1,0:T(8,128)S(1)}, f32[16,256]{1,0:T(8,128)S(1)}, u32[]{:S(2)}, u32[]{:S(2)}) collective-permute-start(f32[16,256]{1,0:T(8,128)S(1)} %get-tuple-element.58), channel_id=1, source_target_pairs={{0,1},{1,2},{2,3},{3,4},{4,5},{5,6},{6,7},{7,8},{8,9},{9,10},{10,1... | collective-permute-start | bytes 49160 | tf_op jit(solution)/shard_map/ppermute | solution.py:72
  72.0 6.0 %collective-permute-start.7 = (f32[16,256]{1,0:T(8,128)S(1)}, f32[16,256]{1,0:T(8,128)S(1)}, u32[]{:S(2)}, u32[]{:S(2)}) collective-permute-start(f32[16,256]{1,0:T(8,128)S(1)} %get-tuple-element.57), channel_id=1, source_target_pairs={{1,0},{2,1},{3,2},{4,3},{5,4},{6,5},{7,6},{8,7},{9,8},{10,9},{11,1... | collective-permute-start | bytes 49160 | tf_op jit(solution)/shard_map/ppermute | solution.py:73
  79.2 8.6 %collective-permute-start.8 = (f32[16,256]{1,0:T(8,128)S(1)}, f32[16,256]{1,0:T(8,128)S(1)}, u32[]{:S(2)}, u32[]{:S(2)}) collective-permute-start(f32[16,256]{1,0:T(8,128)S(1)} %get-tuple-element.56), channel_id=1, source_target_pairs={{0,1},{1,2},{2,3},{3,4},{4,5},{5,6},{6,7},{7,8},{8,9},{9,10},{10,1... | collective-permute-start | bytes 49160 | tf_op jit(solution)/shard_map/ppermute | solution.py:72
  83.2 6.0 %collective-permute-start.9 = (f32[16,256]{1,0:T(8,128)S(1)}, f32[16,256]{1,0:T(8,128)S(1)}, u32[]{:S(2)}, u32[]{:S(2)}) collective-permute-start(f32[16,256]{1,0:T(8,128)S(1)} %get-tuple-element.55), channel_id=1, source_target_pairs={{1,0},{2,1},{3,2},{4,3},{5,4},{6,5},{7,6},{8,7},{9,8},{10,9},{11,1... | collective-permute-start | bytes 49160 | tf_op jit(solution)/shard_map/ppermute | solution.py:73
  90.4 8.6 %collective-permute-start.10 = (f32[16,256]{1,0:T(8,128)S(1)}, f32[16,256]{1,0:T(8,128)S(1)}, u32[]{:S(2)}, u32[]{:S(2)}) collective-permute-start(f32[16,256]{1,0:T(8,128)S(1)} %get-tuple-element.54), channel_id=1, source_target_pairs={{0,1},{1,2},{2,3},{3,4},{4,5},{5,6},{6,7},{7,8},{8,9},{9,10},{10,1... | collective-permute-start | bytes 49160 | tf_op jit(solution)/shard_map/ppermute | solution.py:72
  94.7 5.7 %collective-permute-start.11 = (f32[16,256]{1,0:T(8,128)S(1)}, f32[16,256]{1,0:T(8,128)S(1)}, u32[]{:S(2)}, u32[]{:S(2)}) collective-permute-start(f32[16,256]{1,0:T(8,128)S(1)} %get-tuple-element.53), channel_id=1, source_target_pairs={{1,0},{2,1},{3,2},{4,3},{5,4},{6,5},{7,6},{8,7},{9,8},{10,9},{11,1... | collective-permute-start | bytes 49160 | tf_op jit(solution)/shard_map/ppermute | solution.py:73
  101.0 41.2 %copy-start.2 = (f32[16,1024]{1,0:T(8,128)}, f32[16,1024]{1,0:T(8,128)S(1)}, u32[]{:S(2)}) copy-start(f32[16,1024]{1,0:T(8,128)S(1)} %fusion.40) | copy-start | bytes 196612
  101.1 9.9 %collective-permute-start.12 = (f32[16,1024]{1,0:T(8,128)S(1)}, f32[16,1024]{1,0:T(8,128)S(1)}, u32[]{:S(2)}, u32[]{:S(2)}) collective-permute-start(f32[16,1024]{1,0:T(8,128)S(1)} %fusion.40), channel_id=1, source_target_pairs={{0,128},{16,144},{32,160},{48,176},{64,192},{80,208},{96,224},{112... | collective-permute-start | bytes 196616 | tf_op jit(solution)/shard_map/ppermute | solution.py:111
  111.0 8.8 %collective-permute-start.13 = (f32[2,16,1024]{2,1,0:T(8,128)S(1)}, f32[2,16,1024]{2,1,0:T(8,128)S(1)}, u32[]{:S(2)}, u32[]{:S(2)}) collective-permute-start(f32[2,16,1024]{2,1,0:T(8,128)S(1)} %pad_maximum_fusion.2), channel_id=1, source_target_pairs={{0,64},{16,80},{32,96},{48,112},{64,0},{80,16},{96,32},{112,48},{1... | collective-permute-start | bytes 393224 | tf_op jit(solution)/shard_map/ppermute | solution.py:111
  119.9 9.5 %collective-permute-start.14 = (f32[2,2,16,1024]{3,2,1,0:T(8,128)S(1)}, f32[2,2,16,1024]{3,2,1,0:T(8,128)S(1)}, u32[]{:S(2)}, u32[]{:S(2)}) collective-permute-start(f32[2,2,16,1024]{3,2,1,0:T(8,128)S(1)} %pad_maximum_fusion.1), channel_id=1, source_target_pairs={{0,16},{16,0},{32,48},{48,32},{64,80},{80,64},{96,112},{112,96},{1... | collective-permute-start | bytes 786440 | tf_op jit(solution)/shard_map/ppermute | solution.py:111
  121.1 15.9 %collective-permute-start.16 = (f32[16,256]{1,0:T(8,128)S(1)}, f32[16,256]{1,0:T(8,128)S(1)}, u32[]{:S(2)}, u32[]{:S(2)}) collective-permute-start(f32[16,256]{1,0:T(8,128)S(1)} %get-tuple-element.52), channel_id=1, source_target_pairs={{0,1},{1,2},{2,3},{3,4},{4,5},{5,6},{6,7},{7,8},{8,9},{9,10},{10,1... | collective-permute-start | bytes 49160 | tf_op jit(solution)/shard_map/ppermute | solution.py:72
  129.5 12.7 %collective-permute-start.15 = (f32[2,2,2,16,1024]{4,3,2,1,0:T(8,128)S(1)}, f32[2,2,2,16,1024]{4,3,2,1,0:T(8,128)S(1)}, u32[]{:S(2)}, u32[]{:S(2)}) collective-permute-start(f32[2,2,2,16,1024]{4,3,2,1,0:T(8,128)S(1)} %pad_maximum_fusion), channel_id=1, source_target_pairs={{0,32},{16,48},{32,0},{48,16},{64,96},{80,112},{96,64},{112,80},{1... | collective-permute-start | bytes 1572872 | tf_op jit(solution)/shard_map/ppermute | solution.py:111
  134.1 4.8 %collective-permute-start.17 = (f32[16,256]{1,0:T(8,128)S(1)}, f32[16,256]{1,0:T(8,128)S(1)}, u32[]{:S(2)}, u32[]{:S(2)}) collective-permute-start(f32[16,256]{1,0:T(8,128)S(1)} %get-tuple-element.51), channel_id=1, source_target_pairs={{1,0},{2,1},{3,2},{4,3},{5,4},{6,5},{7,6},{8,7},{9,8},{10,9},{11,1... | collective-permute-start | bytes 49160 | tf_op jit(solution)/shard_map/ppermute | solution.py:73
  143.6 1.3 collective-permute-start.18
  145.0 4.6 %collective-permute-start.19 = (f32[32,1,2,2,16]{0,4,3,2,1:T(8,128)S(1)}, f32[32,1,2,2,16]{0,4,3,2,1:T(8,128)S(1)}, u32[]{:S(2)}, u32[]{:S(2)}) collective-permute-start(f32[32,1,2,2,16]{0,4,3,2,1:T(8,128)S(1)} %select_bitcast_fusion.9), channel_id=1, source_target_pairs={{0,2},{1,3},{2,0},{3,1},{4,6},{5,7},{6,4},{7,5},{8,10},{9,11},{10,... | collective-permute-start | bytes 24584 | tf_op jit(solution)/shard_map/ppermute | solution.py:111
  149.7 3.8 %collective-permute-start.20 = (f32[32,1,1,2,16]{0,4,3,2,1:T(8,128)S(1)}, f32[32,1,1,2,16]{0,4,3,2,1:T(8,128)S(1)}, u32[]{:S(2)}, u32[]{:S(2)}) collective-permute-start(f32[32,1,1,2,16]{0,4,3,2,1:T(8,128)S(1)} %select_bitcast_fusion.10), channel_id=1, source_target_pairs={{0,4},{1,5},{2,6},{3,7},{4,0},{5,1},{6,2},{7,3},{8,12},{9,13},{10,... | collective-permute-start | bytes 12296 | tf_op jit(solution)/shard_map/ppermute | solution.py:111
  153.5 5.2 %collective-permute-start.21 = (f32[32,1,1,1,16]{0,4,3,2,1:T(8,128)S(1)}, f32[32,1,1,1,16]{0,4,3,2,1:T(8,128)S(1)}, u32[]{:S(2)}, u32[]{:S(2)}) collective-permute-start(f32[32,1,1,1,16]{0,4,3,2,1:T(8,128)S(1)} %select_bitcast_fusion.11), channel_id=1, source_target_pairs={{0,8},{1,9},{2,10},{3,11},{4,12},{5,13},{6,14},{7,15},{8,0},{9,1},... | collective-permute-start | bytes 6152 | tf_op jit(solution)/shard_map/ppermute | solution.py:111
  158.8 13.7 %collective-permute-start.22 = (f32[16,16]{0,1:T(8,128)S(1)}, f32[16,16]{0,1:T(8,128)S(1)}, u32[]{:S(2)}, u32[]{:S(2)}) collective-permute-start(f32[16,16]{0,1:T(8,128)S(1)} %get-tuple-element.61), channel_id=1, source_target_pairs={{0,0},{1,16},{2,32},{3,48},{4,64},{5,80},{6,96},{7,112},{8,128},{9... | collective-permute-start | bytes 3080 | tf_op jit(solution)/shard_map/ppermute | solution.py:183

commit v4 on v3

--- a/solution.py
+++ b/solution.py
@@ -145,13 +145,20 @@
     return current
 
 
+def exchange_all(value, axis):
+    count = lax.axis_size(axis)
+    spread = jnp.broadcast_to(value[None], (count,) + value.shape)
+    return lax.all_to_all(spread, axis, 0, 0, tiled=True)
+
+
 def shards(orbitals, potential, stencil, send_list, send_count):
     rows, points = orbitals.shape
     capacity = send_list.shape[1]
     domain_count = lax.axis_size("domain")
     band_count = lax.axis_size("band")
     total_points = points * domain_count
-    extremes = butterfly_max(jnp.stack([-jnp.min(potential), jnp.max(potential)]), "domain")
+    local_extremes = jnp.stack([-jnp.min(potential), jnp.max(potential)])
+    extremes = jnp.max(exchange_all(local_extremes, "domain"), axis=0)
     lowest = -extremes[0]
     highest = extremes[1]
     live_slots = lax.broadcasted_iota(jnp.int32, (2, capacity), 1) < send_count
@@ -167,18 +174,17 @@
 
     filtered = filter_block(orbitals, operator_fn, lowest, highest)
     applied = operator_fn(filtered)
-    band_steps = (8, 4, 1, 2)
-    gathered = gather_blocks(filtered, "band", band_steps)
+    gathered = exchange_all(filtered, "band").reshape(band_count * rows, points)
     both = jnp.stack([filtered, applied])
     parts = jnp.einsum(
-        "srq,abcdjq->srdcabj",
+        "srq,jq->srj",
         both,
         gathered,
         precision=lax.Precision.HIGHEST,
         preferred_element_type=jnp.float32,
     )
-    parts = jnp.transpose(parts, (0, 1, 5, 4, 3, 2, 6)).reshape(2 * rows, 2, 2, 2, 2, rows)
-    sums = scatter_sum(parts, "domain", (1, 2, 4, 8)).reshape(2, rows, rows)
+    blocks = jnp.transpose(parts.reshape(2, rows, domain_count, rows), (2, 0, 1, 3))
+    sums = jnp.sum(lax.all_to_all(blocks, "domain", 0, 0, tiled=True), axis=0)
     swap = [(b * domain_count + d, d * domain_count + b) for b in range(band_count) for d in range(domain_count)]
     mirrored = lax.ppermute(sums[1], ("band", "domain"), swap)
     sums = jnp.stack([sums[0], mirrored.T])

time: 174 us -> 167 us (0.960)
  the two profiles are of different devices: /device:TPU:20 before, /device:TPU:17 now
where the time goes in v4:
time: 167 us; the launch traced here: 166 us
  starting transfers between devices  46.2 us (28%)
  matrix products  34.7 us (21%)
  waiting for transfers between devices  31.1 us (19%)
  other arithmetic  28.8 us (17%)
  blocking collectives  12.1 us (7%)
  local copies, waits for them, and re-layouts  9.96 us (6%)
  between operations  3.3 us (2%)
    dot_general x20, matrix products, dense(): lax.dot_general(left, right, (((1,), (0,)), ((), ())), precision=lax.Prec...  30.3 us
    add x1, other arithmetic, stencil_matrix(): total = total + WEIGHTS[distance + 1] * count  24.2 us
    all_to_all x2, starting transfers between devices, exchange_all(): return lax.all_to_all(spread, axis, 0, 0, tiled=True)  16.5 us
    ppermute x5, starting transfers between devices, apply_operator(): from_below = lax.ppermute(outgoing[:, capacity:], 'domain', forward)  13 us
    all_to_all x2, waiting for transfers between devices, exchange_all(): return lax.all_to_all(spread, axis, 0, 0, tiled=True)  12.9 us
    all_to_all x1, blocking collectives, shards(): sums = jnp.sum(lax.all_to_all(blocks, 'domain', 0, 0, tiled=True), axis=0)  12.1 us
    ppermute x5, starting transfers between devices, apply_operator(): from_above = lax.ppermute(outgoing[:, :capacity], 'domain', backward)  11.6 us
    ppermute x5, waiting for transfers between devices, apply_operator(): from_above = lax.ppermute(outgoing[:, :capacity], 'domain', backward)  9.63 us
  transfers between devices with their start and end apart: 13, of which 6 were waited for; matrix products, arithmetic and copies ran while one was open for 33% of the time, Pallas kernels for 0%

profile of v4, /device:TPU:17, one launch (start us, length us, event | category | flops | bytes accessed | tf_op | source)
XLA Modules:
  0.0 166.0 jit_solution(5057289704157576577)
XLA Ops:
  0.6 0.0 copy-start.3
  0.6 1.3 fusion.59
  2.6 0.7 pad_maximum_fusion
  3.3 0.6 broadcast_in_dim.4
  4.0 6.0 %all-to-all-start = ((f32[16,1,2]{2,1,0:T(1,128)}), f32[16,1,2]{2,1,0:T(1,128)S(1)}, u32[]{:S(2)}, u32[]{:S(2)}) async-start(f32[16,1,2]{2,1,0:T(1,128)} %broadcast_in_dim.4), calls=%async_computation | async-start | bytes 16384 | tf_op jit(solution)/shard_map/all_to_all | solution.py:151
  10.0 0.7 iota_compare_fusion.38
  10.7 0.8 fusion.67
  11.5 0.4 fusion.42
  11.9 0.1 pad_add_fusion
  11.9 1.5 convolution_bitcast_fusion.1
  13.4 3.4 %collective-permute-start = (f32[16,256]{1,0:T(8,128)S(1)}, f32[16,256]{1,0:T(8,128)S(1)}, u32[]{:S(2)}, u32[]{:S(2)}) collective-permute-start(f32[16,256]{1,0:T(8,128)S(1)} %get-tuple-element.63), channel_id=1, source_target_pairs={{0,1},{1,2},{2,3},{3,4},{4,5},{5,6},{6,7},{7,8},{8,9},{9,10},{10,1... | collective-permute-start | bytes 49160 | tf_op jit(solution)/shard_map/ppermute | solution.py:72
  16.8 1.9 %collective-permute-start.1 = (f32[16,256]{1,0:T(8,128)S(1)}, f32[16,256]{1,0:T(8,128)S(1)}, u32[]{:S(2)}, u32[]{:S(2)}) collective-permute-start(f32[16,256]{1,0:T(8,128)S(1)} %get-tuple-element.64), channel_id=1, source_target_pairs={{1,0},{2,1},{3,2},{4,3},{5,4},{6,5},{7,6},{8,7},{9,8},{10,9},{11,1... | collective-permute-start | bytes 49160 | tf_op jit(solution)/shard_map/ppermute | solution.py:73
  18.8 1.3 fusion.61
  20.1 1.4 fusion.60
  21.5 24.2 %multiply_add_fusion = f32[1536,1024]{1,0:T(8,128)S(1)} fusion(s32[1024]{0:T(1024)S(1)} %bitcast.107, s32[1024]{0:T(1024)S(1)} %bitcast.108, s32[1024]{0:T(1024)S(1)} %bitcast.110, s32[1024]{0:T(1024)S(1)} %bitcast.111, s32[1024]{0:T(1024)S(1)} %bitcast.112, s32[1024]{0:T(1024)S(1)} %bitcast.113, s32[1024]{0:T(1024)S(1)} %bitcast.114, s32[1024]{0:T(1024)S(1)} %bitcast.115, ...), kind=kLoop, calls=%fused_computation | loop fusion | flops 177733632 | bytes 6438912 | tf_op jit(solution)/shard_map/add | solution.py:55
  45.7 2.6 %copy-done = f32[1536,1024]{1,0:T(8,128)} copy-done((f32[1536,1024]{1,0:T(8,128)}, f32[1536,1024]{1,0:T(8,128)S(1)}, u32[]{:S(2)}) %copy-start) | copy-done | bytes 6291480
  48.3 2.3 %fusion.10 = f32[16,1024]{1,0:T(8,128)S(1)} fusion(f32[16,1024]{1,0:T(8,128)S(1)} %copy-done.3, f32[1536,1024]{1,0:T(8,128)S(1)} %multiply_add_fusion), kind=kOutput, calls=%fused_computation.49 | convolution fusion | flops 201326592 | bytes 4325376 | tf_op jit(solution)/shard_map/dot_general | solution.py:39
  50.6 0.0 all-to-all-done
  50.7 0.6 fusion.68
  53.0 2.0 %fusion.48 = f32[16,1024]{1,0:T(8,128)S(1)} fusion(f32[16,256]{1,0:T(8,128)S(1)} %collective-permute-done.1, f32[1536,1024]{1,0:T(8,128)} %copy-done), kind=kOutput, calls=%fused_computation.97 | convolution fusion | flops 50331648 | bytes 1130496 | tf_op jit(solution)/shard_map/dot_general | solution.py:39
  54.9 0.0 copy-done.4
  55.0 2.0 %fusion.31 = f32[16,1024]{1,0:T(8,128)S(1)} fusion(f32[16,1024]{1,0:T(8,128)S(1)} %fusion.48, f32[16,1024]{1,0:T(8,128)S(1)} %fusion.10, f32[16,256]{1,0:T(8,128)S(1)} %collective-permute-done, f32[1536,1024]{1,0:T(8,128)} %copy-done, f32[16,1024]{1,0:T(8,128)S(1)} %copy-done.3, f32[]{:T(128)S(6)} %div.43, f32[]{:T(128)S(6)} %div.53, f32[1024]{0:T(1024)S(1)} %copy-done.4), kind=kOutput, calls=%fused_computation.77 | convolution fusion | flops 50495488 | bytes 1331208 | tf_op jit(solution)/shard_map/dot_general | solution.py:39
  56.9 0.6 fusion.69
  57.5 3.6 %collective-permute-start.2 = (f32[16,256]{1,0:T(8,128)S(1)}, f32[16,256]{1,0:T(8,128)S(1)}, u32[]{:S(2)}, u32[]{:S(2)}) collective-permute-start(f32[16,256]{1,0:T(8,128)S(1)} %get-tuple-element.62), channel_id=1, source_target_pairs={{0,1},{1,2},{2,3},{3,4},{4,5},{5,6},{6,7},{7,8},{8,9},{9,10},{10,1... | collective-permute-start | bytes 49160 | tf_op jit(solution)/shard_map/ppermute | solution.py:72
  61.2 4.3 %fusion.6 = f32[16,1024]{1,0:T(8,128)S(1)} fusion(f32[16,1024]{1,0:T(8,128)S(1)} %fusion.31, f32[1536,1024]{1,0:T(8,128)} %copy-done), kind=kOutput, calls=%fused_computation.43 | convolution fusion | flops 201326592 | bytes 4325376 | tf_op jit(solution)/shard_map/dot_general | solution.py:39
  65.5 1.9 %collective-permute-start.3 = (f32[16,256]{1,0:T(8,128)S(1)}, f32[16,256]{1,0:T(8,128)S(1)}, u32[]{:S(2)}, u32[]{:S(2)}) collective-permute-start(f32[16,256]{1,0:T(8,128)S(1)} %get-tuple-element.61), channel_id=1, source_target_pairs={{1,0},{2,1},{3,2},{4,3},{5,4},{6,5},{7,6},{8,7},{9,8},{10,9},{11,1... | collective-permute-start | bytes 49160 | tf_op jit(solution)/shard_map/ppermute | solution.py:73
  67.4 0.6 convolution_add_fusion.7
  68.0 2.5 %collective-permute-done.3 = f32[16,256]{1,0:T(8,128)S(1)} collective-permute-done((f32[16,256]{1,0:T(8,128)S(1)}, f32[16,256]{1,0:T(8,128)S(1)}, u32[]{:S(2)}, u32[]{:S(2)}) %collective-permute-start.3) | collective-permute-done | bytes 16416 | tf_op jit(solution)/shard_map/ppermute | solution.py:73
  70.5 0.6 fusion.34
  71.1 0.6 fusion.70
  71.8 2.1 %collective-permute-start.4 = (f32[16,256]{1,0:T(8,128)S(1)}, f32[16,256]{1,0:T(8,128)S(1)}, u32[]{:S(2)}, u32[]{:S(2)}) collective-permute-start(f32[16,256]{1,0:T(8,128)S(1)} %get-tuple-element.60), channel_id=1, source_target_pairs={{0,1},{1,2},{2,3},{3,4},{4,5},{5,6},{6,7},{7,8},{8,9},{9,10},{10,1... | collective-permute-start | bytes 49160 | tf_op jit(solution)/shard_map/ppermute | solution.py:72
  73.9 2.1 %fusion.4 = f32[16,1024]{1,0:T(8,128)S(1)} fusion(f32[16,1024]{1,0:T(8,128)S(1)} %fusion.34, f32[1536,1024]{1,0:T(8,128)S(1)} %copy-done.1), kind=kOutput, calls=%fused_computation.41 | convolution fusion | flops 201326592 | bytes 4325376 | tf_op jit(solution)/shard_map/dot_general | solution.py:39
  76.0 2.6 %collective-permute-start.5 = (f32[16,256]{1,0:T(8,128)S(1)}, f32[16,256]{1,0:T(8,128)S(1)}, u32[]{:S(2)}, u32[]{:S(2)}) collective-permute-start(f32[16,256]{1,0:T(8,128)S(1)} %get-tuple-element.59), channel_id=1, source_target_pairs={{1,0},{2,1},{3,2},{4,3},{5,4},{6,5},{7,6},{8,7},{9,8},{10,9},{11,1... | collective-permute-start | bytes 49160 | tf_op jit(solution)/shard_map/ppermute | solution.py:73
  78.7 0.6 convolution_add_fusion.5
  79.3 3.1 %collective-permute-done.5 = f32[16,256]{1,0:T(8,128)S(1)} collective-permute-done((f32[16,256]{1,0:T(8,128)S(1)}, f32[16,256]{1,0:T(8,128)S(1)}, u32[]{:S(2)}, u32[]{:S(2)}) %collective-permute-start.5) | collective-permute-done | bytes 16416 | tf_op jit(solution)/shard_map/ppermute | solution.py:73
  82.4 0.6 fusion.37
  83.0 0.6 fusion.71
  83.6 1.9 %collective-permute-start.6 = (f32[16,256]{1,0:T(8,128)S(1)}, f32[16,256]{1,0:T(8,128)S(1)}, u32[]{:S(2)}, u32[]{:S(2)}) collective-permute-start(f32[16,256]{1,0:T(8,128)S(1)} %get-tuple-element.58), channel_id=1, source_target_pairs={{0,1},{1,2},{2,3},{3,4},{4,5},{5,6},{6,7},{7,8},{8,9},{9,10},{10,1... | collective-permute-start | bytes 49160 | tf_op jit(solution)/shard_map/ppermute | solution.py:72
  85.6 2.1 %fusion.2 = f32[16,1024]{1,0:T(8,128)S(1)} fusion(f32[16,1024]{1,0:T(8,128)S(1)} %fusion.37, f32[1536,1024]{1,0:T(8,128)S(1)} %copy-done.1), kind=kOutput, calls=%fused_computation.39 | convolution fusion | flops 201326592 | bytes 4325376 | tf_op jit(solution)/shard_map/dot_general | solution.py:39
  87.7 2.4 %collective-permute-start.7 = (f32[16,256]{1,0:T(8,128)S(1)}, f32[16,256]{1,0:T(8,128)S(1)}, u32[]{:S(2)}, u32[]{:S(2)}) collective-permute-start(f32[16,256]{1,0:T(8,128)S(1)} %get-tuple-element.57), channel_id=1, source_target_pairs={{1,0},{2,1},{3,2},{4,3},{5,4},{6,5},{7,6},{8,7},{9,8},{10,9},{11,1... | collective-permute-start | bytes 49160 | tf_op jit(solution)/shard_map/ppermute | solution.py:73
  90.1 0.6 convolution_add_fusion.3
  90.7 2.9 %collective-permute-done.7 = f32[16,256]{1,0:T(8,128)S(1)} collective-permute-done((f32[16,256]{1,0:T(8,128)S(1)}, f32[16,256]{1,0:T(8,128)S(1)}, u32[]{:S(2)}, u32[]{:S(2)}) %collective-permute-start.7) | collective-permute-done | bytes 16416 | tf_op jit(solution)/shard_map/ppermute | solution.py:73
  93.6 0.6 fusion.40
  94.2 0.0 copy-start.2
  94.2 1.1 broadcast_in_dim.5
  95.3 10.5 %all-to-all-start.1 = ((f32[16,16,1024]{2,1,0:T(8,128)}), f32[16,16,1024]{2,1,0:T(8,128)S(1)}, u32[]{:S(2)}, u32[]{:S(2)}) async-start(f32[16,16,1024]{2,1,0:T(8,128)} %broadcast_in_dim.5), calls=%async_computation.1 | async-start | bytes 2097152 | tf_op jit(solution)/shard_map/all_to_all | solution.py:151
  105.8 0.6 fusion.72
  106.4 1.9 %collective-permute-start.8 = (f32[16,256]{1,0:T(8,128)S(1)}, f32[16,256]{1,0:T(8,128)S(1)}, u32[]{:S(2)}, u32[]{:S(2)}) collective-permute-start(f32[16,256]{1,0:T(8,128)S(1)} %get-tuple-element.56), channel_id=1, source_target_pairs={{0,1},{1,2},{2,3},{3,4},{4,5},{5,6},{6,7},{7,8},{8,9},{9,10},{10,1... | collective-permute-start | bytes 49160 | tf_op jit(solution)/shard_map/ppermute | solution.py:72
  108.4 4.3 %fusion = f32[16,1024]{1,0:T(8,128)S(1)} fusion(f32[16,1024]{1,0:T(8,128)S(1)} %fusion.40, f32[1536,1024]{1,0:T(8,128)} %copy-done), kind=kOutput, calls=%fused_computation.37 | convolution fusion | flops 201326592 | bytes 4325376 | tf_op jit(solution)/shard_map/dot_general | solution.py:39
  112.6 2.7 %collective-permute-start.9 = (f32[16,256]{1,0:T(8,128)S(1)}, f32[16,256]{1,0:T(8,128)S(1)}, u32[]{:S(2)}, u32[]{:S(2)}) collective-permute-start(f32[16,256]{1,0:T(8,128)S(1)} %get-tuple-element.55), channel_id=1, source_target_pairs={{1,0},{2,1},{3,2},{4,3},{5,4},{6,5},{7,6},{8,7},{9,8},{10,9},{11,1... | collective-permute-start | bytes 49160 | tf_op jit(solution)/shard_map/ppermute | solution.py:73
  115.4 1.8 %convolution_add_fusion.1 = f32[16,1024]{1,0:T(8,128)S(1)} fusion(f32[16,1024]{1,0:T(8,128)S(1)} %fusion, f32[16,256]{1,0:T(8,128)S(1)} %collective-permute-done.8, f32[1536,1024]{1,0:T(8,128)} %copy-done), kind=kOutput, calls=%fused_computation.55 | convolution fusion | flops 50348032 | bytes 1196032 | tf_op jit(solution)/shard_map/dot_general | solution.py:39
  117.2 1.1 collective-permute-done.9
  118.3 1.8 %fusion.16 = f32[1,16,1024]{2,1,0:T(8,128)S(1)} fusion(f32[16,1024]{1,0:T(8,128)S(1)} %convolution_add_fusion.1, f32[16,256]{1,0:T(8,128)S(1)} %collective-permute-done.9, f32[1536,1024]{1,0:T(8,128)} %copy-done, f32[16,1024]{1,0:T(8,128)S(1)} %fusion.40, f32[1024]{0:T(1024)S(1)} %copy-done.4), kind=kOutput, calls=%fused_computation.54 | convolution fusion | flops 50429952 | bytes 1265664 | tf_op jit(solution)/shard_map/dot_general | solution.py:39
  120.1 12.9 %all-to-all-done.1 = f32[16,16,1024]{2,1,0:T(8,128)S(1)} async-done(((f32[16,16,1024]{2,1,0:T(8,128)}), f32[16,16,1024]{2,1,0:T(8,128)S(1)}, u32[]{:S(2)}, u32[]{:S(2)}) %all-to-all-start.1) | async-done | bytes 1048608 | tf_op jit(solution)/shard_map/all_to_all | solution.py:151
  133.0 4.4 %convolution_bitcast_fusion = f32[16,2,16,16]{3,2,0,1:T(8,128)S(1)} fusion(f32[16,16,1024]{2,1,0:T(8,128)S(1)} %all-to-all-done.1, f32[1,16,1024]{2,1,0:T(8,128)S(1)} %fusion.16, f32[1,16,1024]{2,1,0:T(8,128)S(1)} %bitcast.91), kind=kOutput, calls=%fused_computation.48 | convolution fusion | flops 100696064 | bytes 1212416 | tf_op jit(solution)/shard_map/srq,jq->srj/dot_general | solution.py:179
  137.5 0.1 reshape.27
  137.6 12.1 %all_to_all.16 = f32[16,1,512]{2,1,0:T(1,128)S(1)} all-to-all(f32[16,1,512]{2,1,0:T(1,128)S(1)} %reshape.27), channel_id=1, replica_groups=mesh['band'=16,'domain'=16] {'domain'}, dimensions={0} | all-to-all | bytes 65536 | tf_op jit(solution)/shard_map/all_to_all | solution.py:187
  149.7 0.5 broadcast.39
  150.2 0.7 reduce.5
  150.9 0.1 reshape.28
  151.1 0.6 slice_bitcast_fusion
  151.7 5.1 %collective-permute-start.10 = (f32[16,16]{1,0:T(8,128)S(1)}, f32[16,16]{1,0:T(8,128)S(1)}, u32[]{:S(2)}, u32[]{:S(2)}) collective-permute-start(f32[16,16]{1,0:T(8,128)S(1)} %get-tuple-element.65), channel_id=1, source_target_pairs={{0,0},{1,16},{2,32},{3,48},{4,64},{5,80},{6,96},{7,112},{8,128},{9... | collective-permute-start | bytes 3080 | tf_op jit(solution)/shard_map/ppermute | solution.py:189
  156.8 8.6 %collective-permute-done.10 = f32[16,16]{1,0:T(8,128)S(1)} collective-permute-done((f32[16,16]{1,0:T(8,128)S(1)}, f32[16,16]{1,0:T(8,128)S(1)}, u32[]{:S(2)}, u32[]{:S(2)}) %collective-permute-start.10) | collective-permute-done | bytes 1056 | tf_op jit(solution)/shard_map/ppermute | solution.py:189
  165.4 0.7 copy.15
  (22 shorter events, 0.2 us)
Async XLA Ops:
  0.6 47.7 %copy-start.3 = (f32[16,1024]{1,0:T(8,128)S(1)}, f32[16,1024]{1,0:T(8,128)}, u32[]{:S(2)}) copy-start(f32[16,1024]{1,0:T(8,128)} %param.5) | copy-start | bytes 196612
  4.0 46.7 %all-to-all-start = ((f32[16,1,2]{2,1,0:T(1,128)}), f32[16,1,2]{2,1,0:T(1,128)S(1)}, u32[]{:S(2)}, u32[]{:S(2)}) async-start(f32[16,1,2]{2,1,0:T(1,128)} %broadcast_in_dim.4), calls=%async_computation | async-start | bytes 16384 | tf_op jit(solution)/shard_map/all_to_all | solution.py:151
  13.4 41.5 %copy-start.4 = (f32[1024]{0:T(1024)S(1)}, f32[1024]{0:T(1024)}, u32[]{:S(2)}) copy-start(f32[1024]{0:T(1024)} %param.6) | copy-start | bytes 12292
  13.4 41.5 %collective-permute-start = (f32[16,256]{1,0:T(8,128)S(1)}, f32[16,256]{1,0:T(8,128)S(1)}, u32[]{:S(2)}, u32[]{:S(2)}) collective-permute-start(f32[16,256]{1,0:T(8,128)S(1)} %get-tuple-element.63), channel_id=1, source_target_pairs={{0,1},{1,2},{2,3},{3,4},{4,5},{5,6},{6,7},{7,8},{8,9},{9,10},{10,1... | collective-permute-start | bytes 49160 | tf_op jit(solution)/shard_map/ppermute | solution.py:72
  16.8 36.1 %collective-permute-start.1 = (f32[16,256]{1,0:T(8,128)S(1)}, f32[16,256]{1,0:T(8,128)S(1)}, u32[]{:S(2)}, u32[]{:S(2)}) collective-permute-start(f32[16,256]{1,0:T(8,128)S(1)} %get-tuple-element.64), channel_id=1, source_target_pairs={{1,0},{2,1},{3,2},{4,3},{5,4},{6,5},{7,6},{8,7},{9,8},{10,9},{11,1... | collective-permute-start | bytes 49160 | tf_op jit(solution)/shard_map/ppermute | solution.py:73
  45.7 2.7 %copy-start = (f32[1536,1024]{1,0:T(8,128)}, f32[1536,1024]{1,0:T(8,128)S(1)}, u32[]{:S(2)}) copy-start(f32[1536,1024]{1,0:T(8,128)S(1)} %multiply_add_fusion) | copy-start | bytes 18874372
  52.9 14.5 %copy-start.1 = (f32[1536,1024]{1,0:T(8,128)S(1)}, f32[1536,1024]{1,0:T(8,128)}, u32[]{:S(2)}) copy-start(f32[1536,1024]{1,0:T(8,128)} %copy-done) | copy-start | bytes 18874372
  57.5 9.9 %collective-permute-start.2 = (f32[16,256]{1,0:T(8,128)S(1)}, f32[16,256]{1,0:T(8,128)S(1)}, u32[]{:S(2)}, u32[]{:S(2)}) collective-permute-start(f32[16,256]{1,0:T(8,128)S(1)} %get-tuple-element.62), channel_id=1, source_target_pairs={{0,1},{1,2},{2,3},{3,4},{4,5},{5,6},{6,7},{7,8},{8,9},{9,10},{10,1... | collective-permute-start | bytes 49160 | tf_op jit(solution)/shard_map/ppermute | solution.py:72
  65.5 5.0 %collective-permute-start.3 = (f32[16,256]{1,0:T(8,128)S(1)}, f32[16,256]{1,0:T(8,128)S(1)}, u32[]{:S(2)}, u32[]{:S(2)}) collective-permute-start(f32[16,256]{1,0:T(8,128)S(1)} %get-tuple-element.61), channel_id=1, source_target_pairs={{1,0},{2,1},{3,2},{4,3},{5,4},{6,5},{7,6},{8,7},{9,8},{10,9},{11,1... | collective-permute-start | bytes 49160 | tf_op jit(solution)/shard_map/ppermute | solution.py:73
  71.8 6.9 %collective-permute-start.4 = (f32[16,256]{1,0:T(8,128)S(1)}, f32[16,256]{1,0:T(8,128)S(1)}, u32[]{:S(2)}, u32[]{:S(2)}) collective-permute-start(f32[16,256]{1,0:T(8,128)S(1)} %get-tuple-element.60), channel_id=1, source_target_pairs={{0,1},{1,2},{2,3},{3,4},{4,5},{5,6},{6,7},{7,8},{8,9},{9,10},{10,1... | collective-permute-start | bytes 49160 | tf_op jit(solution)/shard_map/ppermute | solution.py:72
  76.0 6.4 %collective-permute-start.5 = (f32[16,256]{1,0:T(8,128)S(1)}, f32[16,256]{1,0:T(8,128)S(1)}, u32[]{:S(2)}, u32[]{:S(2)}) collective-permute-start(f32[16,256]{1,0:T(8,128)S(1)} %get-tuple-element.59), channel_id=1, source_target_pairs={{1,0},{2,1},{3,2},{4,3},{5,4},{6,5},{7,6},{8,7},{9,8},{10,9},{11,1... | collective-permute-start | bytes 49160 | tf_op jit(solution)/shard_map/ppermute | solution.py:73
  83.6 6.4 %collective-permute-start.6 = (f32[16,256]{1,0:T(8,128)S(1)}, f32[16,256]{1,0:T(8,128)S(1)}, u32[]{:S(2)}, u32[]{:S(2)}) collective-permute-start(f32[16,256]{1,0:T(8,128)S(1)} %get-tuple-element.58), channel_id=1, source_target_pairs={{0,1},{1,2},{2,3},{3,4},{4,5},{5,6},{6,7},{7,8},{8,9},{9,10},{10,1... | collective-permute-start | bytes 49160 | tf_op jit(solution)/shard_map/ppermute | solution.py:72
  87.7 5.9 %collective-permute-start.7 = (f32[16,256]{1,0:T(8,128)S(1)}, f32[16,256]{1,0:T(8,128)S(1)}, u32[]{:S(2)}, u32[]{:S(2)}) collective-permute-start(f32[16,256]{1,0:T(8,128)S(1)} %get-tuple-element.57), channel_id=1, source_target_pairs={{1,0},{2,1},{3,2},{4,3},{5,4},{6,5},{7,6},{8,7},{9,8},{10,9},{11,1... | collective-permute-start | bytes 49160 | tf_op jit(solution)/shard_map/ppermute | solution.py:73
  94.2 43.2 %copy-start.2 = (f32[16,1024]{1,0:T(8,128)}, f32[16,1024]{1,0:T(8,128)S(1)}, u32[]{:S(2)}) copy-start(f32[16,1024]{1,0:T(8,128)S(1)} %fusion.40) | copy-start | bytes 196612
  95.3 37.7 %all-to-all-start.1 = ((f32[16,16,1024]{2,1,0:T(8,128)}), f32[16,16,1024]{2,1,0:T(8,128)S(1)}, u32[]{:S(2)}, u32[]{:S(2)}) async-start(f32[16,16,1024]{2,1,0:T(8,128)} %broadcast_in_dim.5), calls=%async_computation.1 | async-start | bytes 2097152 | tf_op jit(solution)/shard_map/all_to_all | solution.py:151
  106.4 8.9 %collective-permute-start.8 = (f32[16,256]{1,0:T(8,128)S(1)}, f32[16,256]{1,0:T(8,128)S(1)}, u32[]{:S(2)}, u32[]{:S(2)}) collective-permute-start(f32[16,256]{1,0:T(8,128)S(1)} %get-tuple-element.56), channel_id=1, source_target_pairs={{0,1},{1,2},{2,3},{3,4},{4,5},{5,6},{6,7},{7,8},{8,9},{9,10},{10,1... | collective-permute-start | bytes 49160 | tf_op jit(solution)/shard_map/ppermute | solution.py:72
  112.6 5.7 %collective-permute-start.9 = (f32[16,256]{1,0:T(8,128)S(1)}, f32[16,256]{1,0:T(8,128)S(1)}, u32[]{:S(2)}, u32[]{:S(2)}) collective-permute-start(f32[16,256]{1,0:T(8,128)S(1)} %get-tuple-element.55), channel_id=1, source_target_pairs={{1,0},{2,1},{3,2},{4,3},{5,4},{6,5},{7,6},{8,7},{9,8},{10,9},{11,1... | collective-permute-start | bytes 49160 | tf_op jit(solution)/shard_map/ppermute | solution.py:73
  151.7 13.7 %collective-permute-start.10 = (f32[16,16]{1,0:T(8,128)S(1)}, f32[16,16]{1,0:T(8,128)S(1)}, u32[]{:S(2)}, u32[]{:S(2)}) collective-permute-start(f32[16,16]{1,0:T(8,128)S(1)} %get-tuple-element.65), channel_id=1, source_target_pairs={{0,0},{1,16},{2,32},{3,48},{4,64},{5,80},{6,96},{7,112},{8,128},{9... | collective-permute-start | bytes 3080 | tf_op jit(solution)/shard_map/ppermute | solution.py:189
